TPU v7x, 128 devices: a whole 4x4x4 slice. The times are simulated.
128 devices in a mesh: rep: 16 (over z_lo, x, core), shard: 8 (over z_hi, y).
Axes of the slice: x: 4, y: 4, z: 4 (z_hi: 2, z_lo: 2; z = z_hi * 2 + z_lo), core: 2. Of those that a mesh axis runs over, the one named last changes fastest.
Arguments:
- grad_embed: bfloat16 [16, 8, 4096, 768], P('rep', 'shard'), may hold values from -800 to 800
- grad_proj: bfloat16 [16, 8, 768, 768], P('rep', 'shard'), may hold values from -800 to 800
- grad_norms: bfloat16 [16, 8, 4, 768], P('rep', 'shard'), may hold values from -800 to 800
- embed_master: float32 [4096, 768], P('shard'), may hold values from -0.75 to 0.75
- embed_first: float32 [4096, 768], P('shard'), may hold values from -6 to 6
- embed_second: float32 [4096, 768], P('shard'), may hold values from 0.01 to 4
- proj_master: float32 [768, 768], P('shard'), may hold values from -0.21875 to 0.21875
- proj_first: float32 [768, 768], P('shard'), may hold values from -6 to 6
- proj_second: float32 [768, 768], P('shard'), may hold values from 0.01 to 4
- norm_master: float32 [4, 768], P(None, 'shard'), may hold values from -6 to 6
- norm_first: float32 [4, 768], P(None, 'shard'), may hold values from -6 to 6
- norm_second: float32 [4, 768], P(None, 'shard'), may hold values from 0.01 to 4
Outputs:
- embed_master_new: float32 [4096, 768], P('shard')
- embed_first_new: float32 [4096, 768], P('shard')
- embed_second_new: float32 [4096, 768], P('shard')
- embed_weights: bfloat16 [4096, 768], replicated
- proj_master_new: float32 [768, 768], P('shard')
- proj_first_new: float32 [768, 768], P('shard')
- proj_second_new: float32 [768, 768], P('shard')
- proj_weights: bfloat16 [768, 768], replicated
- norm_master_new: float32 [4, 768], P(None, 'shard')
- norm_first_new: float32 [4, 768], P(None, 'shard')
- norm_second_new: float32 [4, 768], P(None, 'shard')
- norm_weights: bfloat16 [4, 768], replicated
All inputs are finite; a program needn't handle non-finite values.
Results may differ from a plain program's by a relative error of at most 0.0004.
Values may be sent and summed in bfloat16 or wider, within the bound.
No kernel may reach another device: no remote copies, remote signals or barrier semaphores. Data moves between devices by JAX's collectives and lax.ppermute only.
A program may use at most 128 MiB of HBM per device.

v0:
```python
import jax
import jax.numpy as jnp
from jax import lax
from jax.sharding import PartitionSpec as P

beta_one = 0.9
beta_two = 0.95
adam_step = 10.0
adam_eps = 1e-08
learning_rate = 0.002
clip_rms = 1.0

ALL = ("shard", "rep_hi", "core")
HALF = ("shard", "rep_hi")
REP = ("rep_hi", "core")


def adamw(gradient, master, first, second, weight_decay):
    corr_one = 1.0 - beta_one**adam_step
    corr_two = 1.0 - beta_two**adam_step
    first_new = beta_one * first + (1.0 - beta_one) * gradient
    second_new = beta_two * second + (1.0 - beta_two) * gradient * gradient
    direction = (
        first_new / corr_one / (jnp.sqrt(second_new / corr_two) + adam_eps) + weight_decay * master
    )
    master_new = master - learning_rate * direction
    return (master_new, first_new, second_new, master_new.astype(jnp.bfloat16))


def gather_all(piece, axis):
    count = lax.psum(1, axis)
    return lax.all_to_all(
        jnp.broadcast_to(piece[None], (count,) + piece.shape), axis, 0, 0, tiled=True
    )


def shards(
    grad_embed,
    grad_proj,
    grad_norms,
    embed_master,
    embed_first,
    embed_second,
    proj_master,
    proj_first,
    proj_second,
    norm_master,
    norm_first,
    norm_second,
):
    n_rep = lax.psum(1, ("rep_hi", "core"))
    n_shard = lax.psum(1, "shard")
    n_all = n_rep * n_shard
    rep_index = lax.axis_index(("rep_hi", "core"))
    core = lax.axis_index("core")

    embed_rows, width = grad_embed.shape[2:]
    proj_rows = grad_proj.shape[2]
    norm_rows, norm_cols = grad_norms.shape[2:]
    e_rows = embed_rows // n_all
    p_rows = proj_rows // n_all
    n_vals = norm_rows * norm_cols // n_all
    block_norm = norm_cols // n_shard
    rows = e_rows + p_rows + 2
    entry_count = float(embed_rows * width + proj_rows * width + norm_rows * norm_cols)

    embed_send = grad_embed[0, 0].reshape(n_all, e_rows, width)
    proj_send = grad_proj[0, 0].reshape(n_all, p_rows, width)
    norm_send = (
        grad_norms[0, 0]
        .reshape(norm_rows, n_shard, block_norm)
        .transpose(1, 0, 2)
        .reshape(n_all, 1, n_vals)
    )
    norm_send = jnp.pad(norm_send, ((0, 0), (0, 1), (0, width - n_vals)))
    send = jnp.concatenate([embed_send, proj_send, norm_send], axis=1)

    received = lax.all_to_all(send, ALL, 0, 0, tiled=True)
    reduced = jnp.sum(received.astype(jnp.float32), axis=0)

    half_block = gather_all(reduced, "rep_hi")
    half_other = lax.ppermute(half_block, "core", [(0, 1), (1, 0)])
    block = jnp.stack(
        [jnp.where(core == 0, half_block, half_other), jnp.where(core == 0, half_other, half_block)],
        axis=1,
    ).reshape((n_rep,) + reduced.shape)
    embed_sum = block[:, :e_rows].reshape(n_rep * e_rows, width)
    proj_sum = block[:, e_rows : e_rows + p_rows].reshape(n_rep * p_rows, width)
    norm_sum = block[:, e_rows + p_rows, :n_vals].reshape(norm_rows, block_norm)
    partial = jnp.sum(block * block)
    squares = jnp.sum(gather_all(partial.reshape(1), "shard"))
    rms_value = jnp.sqrt(squares / entry_count)
    clip_factor = jnp.minimum(jnp.float32(1.0), clip_rms / (rms_value + 1e-06))

    def flat_norm(x):
        return lax.dynamic_slice(x.reshape(-1), (rep_index * n_vals,), (n_vals,))

    e_piece = adamw(
        clip_factor * reduced[:e_rows],
        lax.dynamic_slice_in_dim(embed_master, rep_index * e_rows, e_rows),
        lax.dynamic_slice_in_dim(embed_first, rep_index * e_rows, e_rows),
        lax.dynamic_slice_in_dim(embed_second, rep_index * e_rows, e_rows),
        0.01,
    )[3]
    p_piece = adamw(
        clip_factor * reduced[e_rows : e_rows + p_rows],
        lax.dynamic_slice_in_dim(proj_master, rep_index * p_rows, p_rows),
        lax.dynamic_slice_in_dim(proj_first, rep_index * p_rows, p_rows),
        lax.dynamic_slice_in_dim(proj_second, rep_index * p_rows, p_rows),
        0.01,
    )[3]
    n_piece = adamw(
        clip_factor * reduced[e_rows + p_rows, :n_vals],
        flat_norm(norm_master),
        flat_norm(norm_first),
        flat_norm(norm_second),
        0.0,
    )[3]
    n_piece = jnp.pad(n_piece.reshape(1, n_vals), ((0, 1), (0, width - n_vals)))
    w_piece = jnp.concatenate([e_piece, p_piece, n_piece], axis=0)
    w_mine = gather_all(w_piece, HALF)
    w_other = lax.ppermute(w_mine, "core", [(0, 1), (1, 0)])

    def interleave(lo, hi):
        mine, other = w_mine[:, lo:hi], w_other[:, lo:hi]
        pair = [jnp.where(core == 0, mine, other), jnp.where(core == 0, other, mine)]
        return jnp.stack(pair, axis=1).reshape((n_all, hi - lo) + w_piece.shape[1:])

    embed_weights = interleave(0, e_rows).reshape(embed_rows, width)
    proj_weights = interleave(e_rows, e_rows + p_rows).reshape(proj_rows, width)
    norm_weights = (
        interleave(e_rows + p_rows, e_rows + p_rows + 1)[:, 0, :n_vals]
        .reshape(n_shard, norm_rows, block_norm)
        .transpose(1, 0, 2)
        .reshape(norm_rows, norm_cols)
    )

    embed_out = adamw(clip_factor * embed_sum, embed_master, embed_first, embed_second, 0.01)
    proj_out = adamw(clip_factor * proj_sum, proj_master, proj_first, proj_second, 0.01)
    norm_out = adamw(clip_factor * norm_sum, norm_master, norm_first, norm_second, 0.0)
    return (
        embed_out[0],
        embed_out[1],
        embed_out[2],
        embed_weights,
        proj_out[0],
        proj_out[1],
        proj_out[2],
        proj_weights,
        norm_out[0],
        norm_out[1],
        norm_out[2],
        norm_weights,
    )


def solution(mesh):
    n_rep, n_shard = mesh.devices.shape
    fine = jax.sharding.Mesh(
        mesh.devices.reshape(n_rep // 2, 2, n_shard), ("rep_hi", "core", "shard")
    )
    rep = ("rep_hi", "core")
    return jax.shard_map(
        shards,
        mesh=fine,
        in_specs=(
            P(rep, "shard", None, None),
            P(rep, "shard", None, None),
            P(rep, "shard", None, None),
            P("shard", None),
            P("shard", None),
            P("shard", None),
            P("shard", None),
            P("shard", None),
            P("shard", None),
            P(None, "shard"),
            P(None, "shard"),
            P(None, "shard"),
        ),
        out_specs=(
            P("shard", None),
            P("shard", None),
            P("shard", None),
            P(),
            P("shard", None),
            P("shard", None),
            P("shard", None),
            P(),
            P(None, "shard"),
            P(None, "shard"),
            P(None, "shard"),
            P(),
        ),
        check_vma=False,
    )
```

profile of v0, /device:TPU:1, one launch (start us, length us, event | category | flops | bytes accessed | tf_op | source)
XLA Modules:
  0.0 229.6 jit_solution(15090279926273857746)
XLA Ops:
  0.7 2.2 reshape_squeeze.14
  2.9 0.1 reshape_squeeze.15
  3.0 0.1 reshape.74
  3.1 3.8 %fusion.1 = bf16[128,40,768]{2,1,0:T(8,128)(2,1)S(1)} fusion(bf16[128,1,24]{2,1,0:T(2,128)(2,1)S(1)} %reshape.74, bf16[128,6,768]{2,1,0:T(8,128)(2,1)S(1)} %reshape_squeeze.14, bf16[128,32,768]{2,1,0:T(8,128)(2,1)} %bitcast.50), kind=kLoop, calls=%fused_computation.3 | loop fusion | flops 31457280 | bytes 15341568 | tf_op jit(solution)/shard_map/concatenate | solution.py:76
  6.9 103.4 %all_to_all.21 = bf16[128,40,768]{2,1,0:T(8,128)(2,1)S(1)} all-to-all(bf16[128,40,768]{2,1,0:T(8,128)(2,1)S(1)} %fusion.1), channel_id=1, replica_groups=mesh['rep_hi'=8,'core'=2,'shard'=8] {'shard','rep_hi','core'}, dimensions={0} | all-to-all | bytes 15728640 | tf_op jit(solution)/shard_map/all_to_all | solution.py:78
  110.3 1.1 convert_reduce_fusion
  111.4 0.0 copy-start.6
  111.4 0.0 copy-start.5
  111.4 0.0 copy-start.4
  111.5 0.1 broadcast_in_dim.6
  111.5 18.0 %all_to_all.22 = f32[8,40,768]{2,1,0:T(8,128)S(1)} all-to-all(f32[8,40,768]{2,1,0:T(8,128)S(1)} %broadcast_in_dim.6), channel_id=1, replica_groups=mesh['rep_hi'=8,'core'=2,'shard'=8] {'rep_hi'}, dimensions={0} | all-to-all | bytes 1966080 | tf_op jit(solution)/shard_map/all_to_all | solution.py:32
  129.5 1.6 collective-permute-start
  131.1 0.1 reshape.68
  131.2 0.1 reshape.69
  131.3 0.7 reshape.70
  131.9 1.4 collective-permute-done
  133.3 0.1 select_bitcast_fusion.3
  133.4 0.0 copy-start
  133.4 1.1 multiply_reduce_fusion
  134.5 0.6 broadcast_in_dim.7
  135.2 10.8 %all_to_all.23 = f32[8,1,1]{2,1,0:T(1,128)S(1)} all-to-all(f32[8,1,1]{2,1,0:T(1,128)S(1)} %broadcast_in_dim.7), channel_id=1, replica_groups=mesh['rep_hi'=8,'core'=2,'shard'=8] {'shard'}, dimensions={0} | all-to-all | bytes 64 | tf_op jit(solution)/shard_map/all_to_all | solution.py:32
  146.0 0.6 reduce_sum.29
  147.4 1.1 subtract_convert_fusion
  148.5 0.9 subtract_convert_fusion.1
  149.4 0.8 convert_bitcast_fusion
  150.2 0.3 broadcast_in_dim.8
  150.5 52.9 %all_to_all.24 = bf16[64,40,768]{2,1,0:T(8,128)(2,1)} all-to-all(bf16[64,40,768]{2,1,0:T(8,128)(2,1)S(1)} %broadcast_in_dim.8), channel_id=1, replica_groups=mesh['rep_hi'=8,'core'=2,'shard'=8] {'shard','rep_hi'}, dimensions={0} | all-to-all | bytes 7864320 | tf_op jit(solution)/shard_map/all_to_all | solution.py:32
  203.4 2.4 %collective-permute-start.1 = (bf16[64,40,768]{2,1,0:T(8,128)(2,1)}, bf16[64,40,768]{2,1,0:T(8,128)(2,1)}, u32[]{:S(2)}, u32[]{:S(2)}) collective-permute-start(bf16[64,40,768]{2,1,0:T(8,128)(2,1)} %all_to_all.24), channel_id=1, source_target_pairs={{0,8},{8,0},{1,9},{9,1},{2,10},{10,2},{3,11},{11,3},{4,12},{12,4},... | collective-permute-start | bytes 11796488 | tf_op jit(solution)/shard_map/ppermute | solution.py:122
  205.8 0.8 slice_multiply_fusion.1
  206.6 1.8 mul.351
  208.4 0.1 mul.367
  208.5 1.3 multiply_subtract_fusion.2
  209.8 2.3 multiply_subtract_fusion.1
  212.1 0.2 slice_multiply_fusion
  212.2 1.2 copy-done.1
  213.5 0.5 copy-done.2
  213.9 3.0 %multiply_subtract_fusion = (f32[512,768]{1,0:T(8,128)}, f32[512,768]{1,0:T(8,128)}, f32[512,768]{1,0:T(8,128)}) fusion(f32[512,768]{1,0:T(8,128)S(1)} %copy-done, f32[16,32,768]{2,1,0:T(8,128)S(1)} %slice_multiply_fusion, f32[512,768]{1,0:T(8,128)S(1)} %copy-done.1, f32[512,768]{1,0:T(8,128)S(1)} %copy-done.2), kind=kLoop, calls=%fused_computation.15 | loop fusion | flops 5898240 | bytes 11010048 | tf_op jit(solution)/shard_map/sub | solution.py:26
  216.9 2.0 broadcast_select_fusion.1
  219.0 0.2 copy.67
  219.2 0.1 reshape.72
  219.3 0.1 reshape_squeeze.16
  219.4 0.7 reshape.73
  220.0 1.5 select_bitcast_fusion.5
  221.5 0.4 pad_maximum_fusion.2
  221.9 0.1 copy.66
  222.0 1.2 reshape_reshape.7
  223.3 3.1 %select_bitcast_fusion.1 = (bf16[64,1,32,768]{3,2,1,0:T(8,128)(2,1)S(1)}, bf16[64,1,32,768]{3,2,1,0:T(8,128)(2,1)S(1)}) fusion(pred[]{:T(512)S(6)} %eq.2, bf16[64,40,768]{2,1,0:T(8,128)(2,1)} %collective-permute-done.1, bf16[64,40,768]{2,1,0:T(8,128)(2,1)} %all_to_all.24), kind=kLoop, calls=%fused_computation.6 | loop fusion | flops 3145728 | bytes 12582913 | tf_op jit(solution)/shard_map/stack | solution.py:127
  226.3 3.3 %pad_maximum_fusion = bf16[64,2,32,768]{3,2,1,0:T(8,128)(2,1)} fusion(bf16[64,1,32,768]{3,2,1,0:T(8,128)(2,1)S(1)} %get-tuple-element.26, bf16[64,1,32,768]{3,2,1,0:T(8,128)(2,1)S(1)} %get-tuple-element.25), kind=kLoop, calls=%fused_computation.4 | loop fusion | flops 3145728 | bytes 12582912 | tf_op jit(solution)/shard_map/stack | solution.py:127
  (18 shorter events, 0.1 us)
Async XLA Ops:
  0.6 2.3 copy-start.7
  111.4 18.1 %copy-start.3 = (f32[40,768]{1,0:T(8,128)}, f32[40,768]{1,0:T(8,128)S(1)}, u32[]{:S(2)}) copy-start(f32[40,768]{1,0:T(8,128)S(1)} %convert_reduce_fusion) | copy-start | bytes 368644
  111.4 19.7 %copy-start.6 = (f32[4,96]{1,0:T(4,128)S(1)}, f32[4,96]{1,0:T(4,128)}, u32[]{:S(2)}) copy-start(f32[4,96]{1,0:T(4,128)} %param.21) | copy-start | bytes 4612
  111.4 19.7 %copy-start.5 = (f32[4,96]{1,0:T(4,128)S(1)}, f32[4,96]{1,0:T(4,128)}, u32[]{:S(2)}) copy-start(f32[4,96]{1,0:T(4,128)} %param.22) | copy-start | bytes 4612
  111.4 19.8 %copy-start.4 = (f32[4,96]{1,0:T(4,128)S(1)}, f32[4,96]{1,0:T(4,128)}, u32[]{:S(2)}) copy-start(f32[4,96]{1,0:T(4,128)} %param.23) | copy-start | bytes 4612
  129.5 3.8 %collective-permute-start = (f32[8,40,768]{2,1,0:T(8,128)S(1)}, f32[8,40,768]{2,1,0:T(8,128)S(1)}, u32[]{:S(2)}, u32[]{:S(2)}) collective-permute-start(f32[8,40,768]{2,1,0:T(8,128)S(1)} %all_to_all.22), channel_id=1, source_target_pairs={{0,8},{8,0},{1,9},{9,1},{2,10},{10,2},{3,11},{11,3},{4,12},{12,4},... | collective-permute-start | bytes 2949128 | tf_op jit(solution)/shard_map/ppermute | solution.py:82
  133.4 14.0 %copy-start = (f32[512,768]{1,0:T(8,128)S(1)}, f32[512,768]{1,0:T(8,128)}, u32[]{:S(2)}) copy-start(f32[512,768]{1,0:T(8,128)} %param.15) | copy-start | bytes 4718596
  203.4 13.5 %collective-permute-start.1 = (bf16[64,40,768]{2,1,0:T(8,128)(2,1)}, bf16[64,40,768]{2,1,0:T(8,128)(2,1)}, u32[]{:S(2)}, u32[]{:S(2)}) collective-permute-start(bf16[64,40,768]{2,1,0:T(8,128)(2,1)} %all_to_all.24), channel_id=1, source_target_pairs={{0,8},{8,0},{1,9},{9,1},{2,10},{10,2},{3,11},{11,3},{4,12},{12,4},... | collective-permute-start | bytes 11796488 | tf_op jit(solution)/shard_map/ppermute | solution.py:122
  212.1 1.4 copy-start.1
  212.1 1.9 copy-start.2
where the time goes:
time: 230 us
  blocking collectives  185 us (80%)
  other arithmetic  27.3 us (12%)
  local copies, waits for them, and re-layouts  10.2 us (4%)
  starting transfers between devices  3.99 us (2%)
    all_to_all x1, blocking collectives, shards(): received = lax.all_to_all(send, ALL, 0, 0, tiled=True)  103 us
    all_to_all x3, blocking collectives, gather_all(): lax.all_to_all(jnp.broadcast_to(piece[None], (count,) + piece.shape), axi...  81.8 us
    another operation x5, other arithmetic, interleave(): return jnp.stack(pair, axis=1).reshape((n_all, hi - lo) + w_piece.shape[1:])  8.22 us
    sub x3, other arithmetic, adamw(): master_new = master - learning_rate * direction  6.54 us
  transfers between devices with their start and end apart: 2, of which 1 were waited for; matrix products, arithmetic and copies ran while one was open for 4% of the time, Pallas kernels for 0%

commit v1 on v0

--- a/solution.py
+++ b/solution.py
@@ -75,15 +75,17 @@
     norm_send = jnp.pad(norm_send, ((0, 0), (0, 1), (0, width - n_vals)))
     send = jnp.concatenate([embed_send, proj_send, norm_send], axis=1)
 
+    def by_core(mine, other):
+        shape = (mine.shape[0], 2) + mine.shape[1:]
+        slot = lax.broadcasted_iota(jnp.int32, shape, 1)
+        return jnp.where(slot == core, mine[:, None], other[:, None])
+
     received = lax.all_to_all(send, ALL, 0, 0, tiled=True)
     reduced = jnp.sum(received.astype(jnp.float32), axis=0)
 
     half_block = gather_all(reduced, "rep_hi")
     half_other = lax.ppermute(half_block, "core", [(0, 1), (1, 0)])
-    block = jnp.stack(
-        [jnp.where(core == 0, half_block, half_other), jnp.where(core == 0, half_other, half_block)],
-        axis=1,
-    ).reshape((n_rep,) + reduced.shape)
+    block = by_core(half_block, half_other).reshape((n_rep,) + reduced.shape)
     embed_sum = block[:, :e_rows].reshape(n_rep * e_rows, width)
     proj_sum = block[:, e_rows : e_rows + p_rows].reshape(n_rep * p_rows, width)
     norm_sum = block[:, e_rows + p_rows, :n_vals].reshape(norm_rows, block_norm)
@@ -122,9 +124,9 @@
     w_other = lax.ppermute(w_mine, "core", [(0, 1), (1, 0)])
 
     def interleave(lo, hi):
-        mine, other = w_mine[:, lo:hi], w_other[:, lo:hi]
-        pair = [jnp.where(core == 0, mine, other), jnp.where(core == 0, other, mine)]
-        return jnp.stack(pair, axis=1).reshape((n_all, hi - lo) + w_piece.shape[1:])
+        return by_core(w_mine[:, lo:hi], w_other[:, lo:hi]).reshape(
+            (n_all, hi - lo) + w_piece.shape[1:]
+        )
 
     embed_weights = interleave(0, e_rows).reshape(embed_rows, width)
     proj_weights = interleave(e_rows, e_rows + p_rows).reshape(proj_rows, width)

time: 230 us -> 237 us (1.030)
  local copies, waits for them, and re-layouts: 10.2 us -> 23.4 us
  other arithmetic: 27.3 us -> 20.3 us
    another operation x6 -> x0, other arithmetic: 8.36 us -> none  [the longest x5 8.22 us: interleave(): return jnp.stack(pair, axis=1).reshape((n_all, hi - lo) + w_piece.shape[1:])]
    slice x1 -> x8, local copies, waits for them, and re-layouts: 0.01 us -> 6.5 us  [the longest x4 5.38 us: interleave(): w_other[:, lo:hi]]
    broadcast_in_dim x0 -> x10, local copies, waits for them, and re-layouts: none -> 4.79 us  [by_core(): return jnp.where(slot == core, mine[:, None], other[:, None])]
    select_n x1 -> x4, other arithmetic: 1.99 us -> 6.69 us  [by_core(): return jnp.where(slot == core, mine[:, None], other[:, None])]
    all_to_all x0 -> x1, local copies, waits for them, and re-layouts: none -> 3.21 us  [gather_all(): lax.all_to_all(jnp.broadcast_to(piece[None], (count,) + piece.shape), axi...]
  transfers between devices with their start and end apart: 2 -> 2, of which waited for: 1 -> 1; matrix products, arithmetic and copies ran while one was open for 4% -> 5% of each run, Pallas kernels for 0% -> 0%
where the time goes in v1:
time: 237 us; the launch traced here: 236 us
  blocking collectives  184 us (78%)
  local copies, waits for them, and re-layouts  23.4 us (10%)
  other arithmetic  20.3 us (9%)
  starting transfers between devices  4.01 us (2%)
    all_to_all x1, blocking collectives, shards(): received = lax.all_to_all(send, ALL, 0, 0, tiled=True)  103 us
    all_to_all x3, blocking collectives, gather_all(): lax.all_to_all(jnp.broadcast_to(piece[None], (count,) + piece.shape), axi...  81.1 us
    select_n x4, other arithmetic, by_core(): return jnp.where(slot == core, mine[:, None], other[:, None])  6.69 us
    slice x4, local copies, waits for them, and re-layouts, interleave(): w_other[:, lo:hi]  5.38 us
    broadcast_in_dim x10, local copies, waits for them, and re-layouts, by_core(): return jnp.where(slot == core, mine[:, None], other[:, None])  4.79 us
  transfers between devices with their start and end apart: 2, of which 1 were waited for; matrix products, arithmetic and copies ran while one was open for 5% of the time, Pallas kernels for 0%

profile of v1, /device:TPU:1, one launch (start us, length us, event | category | flops | bytes accessed | tf_op | source)
XLA Modules:
  0.0 235.8 jit_solution(879578260741729104)
XLA Ops:
  0.7 2.2 reshape_squeeze.14
  3.1 3.8 %fusion.1 = bf16[128,40,768]{2,1,0:T(8,128)(2,1)S(1)} fusion(bf16[128,1,24]{2,1,0:T(2,128)(2,1)S(1)} %reshape.135, bf16[128,6,768]{2,1,0:T(8,128)(2,1)S(1)} %reshape_squeeze.14, bf16[128,32,768]{2,1,0:T(8,128)(2,1)} %bitcast.34), kind=kLoop, calls=%fused_computation.3 | loop fusion | flops 31457280 | bytes 15341568 | tf_op jit(solution)/shard_map/concatenate | solution.py:76
  6.9 103.4 %all_to_all.21 = bf16[128,40,768]{2,1,0:T(8,128)(2,1)S(1)} all-to-all(bf16[128,40,768]{2,1,0:T(8,128)(2,1)S(1)} %fusion.1), channel_id=1, replica_groups=mesh['rep_hi'=8,'core'=2,'shard'=8] {'shard','rep_hi','core'}, dimensions={0} | all-to-all | bytes 15728640 | tf_op jit(solution)/shard_map/all_to_all | solution.py:83
  110.3 1.1 convert_reduce_fusion
  111.5 18.0 %all_to_all.22 = f32[8,40,768]{2,1,0:T(8,128)S(1)} all-to-all(f32[8,40,768]{2,1,0:T(8,128)S(1)} %broadcast_in_dim.109), channel_id=1, replica_groups=mesh['rep_hi'=8,'core'=2,'shard'=8] {'rep_hi'}, dimensions={0} | all-to-all | bytes 1966080 | tf_op jit(solution)/shard_map/all_to_all | solution.py:32
  129.5 1.6 collective-permute-start
  131.3 1.9 collective-permute-done
  133.3 1.2 multiply_reduce_fusion
  134.5 0.6 broadcast_in_dim.112
  135.1 10.8 %all_to_all.23 = f32[8,1,1]{2,1,0:T(1,128)S(1)} all-to-all(f32[8,1,1]{2,1,0:T(1,128)S(1)} %broadcast_in_dim.112), channel_id=1, replica_groups=mesh['rep_hi'=8,'core'=2,'shard'=8] {'shard'}, dimensions={0} | all-to-all | bytes 64 | tf_op jit(solution)/shard_map/all_to_all | solution.py:32
  146.0 0.6 reduce_sum.29
  147.3 1.1 subtract_convert_fusion
  148.4 0.9 subtract_convert_fusion.1
  149.4 0.3 broadcast_in_dim.115
  149.6 52.2 %all_to_all.24 = bf16[64,40,768]{2,1,0:T(8,128)(2,1)S(1)} all-to-all(bf16[64,40,768]{2,1,0:T(8,128)(2,1)S(1)} %broadcast_in_dim.115), channel_id=1, replica_groups=mesh['rep_hi'=8,'core'=2,'shard'=8] {'shard','rep_hi'}, dimensions={0} | all-to-all | bytes 7864320 | tf_op jit(solution)/shard_map/all_to_all | solution.py:32
  201.9 3.2 %copy.56 = bf16[64,40,768]{2,0,1:T(8,128)(2,1)} copy(bf16[64,40,768]{2,1,0:T(8,128)(2,1)S(1)} %all_to_all.24) | data formatting | bytes 7864320 | tf_op jit(solution)/shard_map/all_to_all | solution.py:32
  205.1 2.5 %collective-permute-start.1 = (bf16[64,40,768]{2,0,1:T(8,128)(2,1)}, bf16[64,40,768]{2,0,1:T(8,128)(2,1)}, u32[]{:S(2)}, u32[]{:S(2)}) collective-permute-start(bf16[64,40,768]{2,0,1:T(8,128)(2,1)} %copy.56), channel_id=1, source_target_pairs={{0,8},{8,0},{1,9},{9,1},{2,10},{10,2},{3,11},{11,3},{4,12},{12,4},... | collective-permute-start | bytes 11796488 | tf_op jit(solution)/shard_map/ppermute | solution.py:124
  207.6 0.7 iota.48
  208.3 0.7 iota.45
  209.2 0.1 iota.42
  209.3 0.6 iota.39
  209.9 1.4 bitcast_select_fusion.1
  211.5 0.6 multiply_subtract_fusion.2
  212.1 0.1 copy-done.8
  212.3 1.0 multiply_subtract_fusion.1
  213.3 0.2 slice_multiply_fusion
  213.5 0.5 copy-done.5
  214.0 0.8 copy-done.3
  214.8 0.5 copy-done.4
  215.3 3.0 %multiply_subtract_fusion = (f32[512,768]{1,0:T(8,128)}, f32[512,768]{1,0:T(8,128)}, f32[512,768]{1,0:T(8,128)}) fusion(f32[512,768]{1,0:T(8,128)S(1)} %copy-done.3, f32[16,32,768]{2,1,0:T(8,128)S(1)} %slice_multiply_fusion, f32[512,768]{1,0:T(8,128)S(1)} %copy-done.4, f32[512,768]{1,0:T(8,128)S(1)} %copy-done.5), kind=kLoop, calls=%fused_computation.12 | loop fusion | flops 5898240 | bytes 11010048 | tf_op jit(solution)/shard_map/sub | solution.py:26
  218.3 1.0 slice_bitcast_fusion.1
  219.3 0.1 broadcast_in_dim.125
  219.4 0.8 broadcast_in_dim.126
  220.1 0.1 broadcast_in_dim.120
  220.2 0.4 broadcast_in_dim.121
  220.7 0.9 slice_bitcast_fusion
  221.6 0.1 broadcast_in_dim.128
  221.8 0.8 slice_select_fusion
  222.7 0.7 reshape.134
  223.4 1.1 slice.60
  224.5 0.3 copy.58
  224.9 0.1 broadcast_in_dim.122
  225.0 1.2 broadcast_in_dim.123
  226.2 2.2 slice.57
  228.5 1.7 copy.57
  230.2 1.2 broadcast_select_fusion
  231.4 1.1 slice-done.1
  232.5 3.2 %bitcast_select_fusion = bf16[4096,768]{1,0:T(8,128)(2,1)} fusion(pred[4096]{0:T(1024)(128)(4,1)S(1)} %iota.42, bf16[64,32,768]{2,1,0:T(8,128)(2,1)S(1)} %copy.57, bf16[64,32,768]{2,1,0:T(8,128)(2,1)S(1)} %slice-done.1), kind=kLoop, calls=%fused_computation.4 | loop fusion | flops 3145728 | bytes 12587008 | tf_op jit(solution)/shard_map/jit(_where)/select_n | solution.py:81
  (51 shorter events, 1.2 us)
Async XLA Ops:
  0.6 2.3 copy-start.12
  111.4 19.7 %copy-start.11 = (f32[4,96]{1,0:T(4,128)S(1)}, f32[4,96]{1,0:T(4,128)}, u32[]{:S(2)}) copy-start(f32[4,96]{1,0:T(4,128)} %param.21) | copy-start | bytes 4612
  111.4 19.7 %copy-start.10 = (f32[4,96]{1,0:T(4,128)S(1)}, f32[4,96]{1,0:T(4,128)}, u32[]{:S(2)}) copy-start(f32[4,96]{1,0:T(4,128)} %param.22) | copy-start | bytes 4612
  111.4 19.8 %copy-start.9 = (f32[4,96]{1,0:T(4,128)S(1)}, f32[4,96]{1,0:T(4,128)}, u32[]{:S(2)}) copy-start(f32[4,96]{1,0:T(4,128)} %param.23) | copy-start | bytes 4612
  129.5 18.9 %copy-start.6 = (f32[96,768]{1,0:T(8,128)S(1)}, f32[96,768]{1,0:T(8,128)}, u32[]{:S(2)}) copy-start(f32[96,768]{1,0:T(8,128)} %param.20) | copy-start | bytes 884740
  129.5 18.9 %copy-start.7 = (f32[96,768]{1,0:T(8,128)S(1)}, f32[96,768]{1,0:T(8,128)}, u32[]{:S(2)}) copy-start(f32[96,768]{1,0:T(8,128)} %param.19) | copy-start | bytes 884740
  129.5 3.8 %collective-permute-start = (f32[8,40,768]{2,1,0:T(8,128)S(1)}, f32[8,40,768]{2,1,0:T(8,128)S(1)}, u32[]{:S(2)}, u32[]{:S(2)}) collective-permute-start(f32[8,40,768]{2,1,0:T(8,128)S(1)} %all_to_all.22), channel_id=1, source_target_pairs={{0,8},{8,0},{1,9},{9,1},{2,10},{10,2},{3,11},{11,3},{4,12},{12,4},... | collective-permute-start | bytes 2949128 | tf_op jit(solution)/shard_map/ppermute | solution.py:87
  133.3 16.4 %copy-start.2 = (f32[8,40,768]{2,1,0:T(8,128)}, f32[8,40,768]{2,1,0:T(8,128)S(1)}, u32[]{:S(2)}) copy-start(f32[8,40,768]{2,1,0:T(8,128)S(1)} %collective-permute-done) | copy-start | bytes 2949124
  201.9 3.2 %copy-start = (bf16[64,40,768]{2,1,0:T(8,128)(2,1)}, bf16[64,40,768]{2,1,0:T(8,128)(2,1)S(1)}, u32[]{:S(2)}) copy-start(bf16[64,40,768]{2,1,0:T(8,128)(2,1)S(1)} %all_to_all.24) | copy-start | bytes 11796484
  205.1 15.6 %collective-permute-start.1 = (bf16[64,40,768]{2,0,1:T(8,128)(2,1)}, bf16[64,40,768]{2,0,1:T(8,128)(2,1)}, u32[]{:S(2)}, u32[]{:S(2)}) collective-permute-start(bf16[64,40,768]{2,0,1:T(8,128)(2,1)} %copy.56), channel_id=1, source_target_pairs={{0,8},{8,0},{1,9},{9,1},{2,10},{10,2},{3,11},{11,3},{4,12},{12,4},... | collective-permute-start | bytes 11796488 | tf_op jit(solution)/shard_map/ppermute | solution.py:124
  211.3 1.0 copy-start.8
  212.3 1.7 copy-start.5
  213.3 1.5 copy-start.3
  213.3 2.0 copy-start.4
  218.3 1.8 slice-start
  220.7 1.1 copy-start.14
  228.4 1.8 copy-start.1
  228.4 1.8 copy-start.13
  230.2 2.3 slice-start.1

commit v2 on v0

--- a/solution.py
+++ b/solution.py
@@ -122,9 +122,13 @@
     w_other = lax.ppermute(w_mine, "core", [(0, 1), (1, 0)])
 
     def interleave(lo, hi):
-        mine, other = w_mine[:, lo:hi], w_other[:, lo:hi]
-        pair = [jnp.where(core == 0, mine, other), jnp.where(core == 0, other, mine)]
-        return jnp.stack(pair, axis=1).reshape((n_all, hi - lo) + w_piece.shape[1:])
+        mine, other = w_mine[:, None, lo:hi], w_other[:, None, lo:hi]
+        pair = jnp.where(
+            core == 0,
+            jnp.concatenate([mine, other], axis=1),
+            jnp.concatenate([other, mine], axis=1),
+        )
+        return pair.reshape((n_all, hi - lo) + w_piece.shape[1:])
 
     embed_weights = interleave(0, e_rows).reshape(embed_rows, width)
     proj_weights = interleave(e_rows, e_rows + p_rows).reshape(proj_rows, width)

time: 230 us -> 237 us (1.030)
  local copies, waits for them, and re-layouts: 10.2 us -> 23.7 us
  other arithmetic: 27.3 us -> 20.7 us
    another operation x5 -> x0, other arithmetic: 8.22 us -> none  [interleave(): return jnp.stack(pair, axis=1).reshape((n_all, hi - lo) + w_piece.shape[1:])]
    broadcast_in_dim x0 -> x4, local copies, waits for them, and re-layouts: none -> 7.52 us  [interleave(): mine, other = (w_mine[:, None, lo:hi], w_other[:, None, lo:hi])]
    select_n x0 -> x4, local copies, waits for them, and re-layouts: none -> 4.75 us  [interleave(): jnp.where(core == 0, jnp.concatenate([mine, other], axis=1), jnp.concaten...]
    slice x0 -> x2, local copies, waits for them, and re-layouts: none -> 2.68 us  [interleave(): mine, other = (w_mine[:, None, lo:hi], w_other[:, None, lo:hi])]
  transfers between devices with their start and end apart: 2 -> 2, of which waited for: 1 -> 1; matrix products, arithmetic and copies ran while one was open for 4% -> 7% of each run, Pallas kernels for 0% -> 0%
where the time goes in v2:
time: 237 us; the launch traced here: 236 us
  blocking collectives  185 us (78%)
  local copies, waits for them, and re-layouts  23.7 us (10%)
  other arithmetic  20.7 us (9%)
  starting transfers between devices  3.99 us (2%)
    all_to_all x1, blocking collectives, shards(): received = lax.all_to_all(send, ALL, 0, 0, tiled=True)  103 us
    all_to_all x3, blocking collectives, gather_all(): lax.all_to_all(jnp.broadcast_to(piece[None], (count,) + piece.shape), axi...  81.8 us
    broadcast_in_dim x4, local copies, waits for them, and re-layouts, interleave(): mine, other = (w_mine[:, None, lo:hi], w_other[:, None, lo:hi])  7.52 us
    sub x3, other arithmetic, adamw(): master_new = master - learning_rate * direction  6.54 us
    select_n x4, local copies, waits for them, and re-layouts, interleave(): jnp.where(core == 0, jnp.concatenate([mine, other], axis=1), jnp.concaten...  4.75 us
  transfers between devices with their start and end apart: 2, of which 1 were waited for; matrix products, arithmetic and copies ran while one was open for 7% of the time, Pallas kernels for 0%

profile of v2, /device:TPU:1, one launch (start us, length us, event | category | flops | bytes accessed | tf_op | source)
XLA Modules:
  0.0 236.5 jit_solution(10393035412436581866)
XLA Ops:
  0.7 2.2 reshape_squeeze.14
  2.9 0.1 reshape_squeeze.15
  3.0 0.1 reshape.115
  3.1 3.8 %fusion.1 = bf16[128,40,768]{2,1,0:T(8,128)(2,1)S(1)} fusion(bf16[128,1,24]{2,1,0:T(2,128)(2,1)S(1)} %reshape.115, bf16[128,6,768]{2,1,0:T(8,128)(2,1)S(1)} %reshape_squeeze.14, bf16[128,32,768]{2,1,0:T(8,128)(2,1)} %bitcast.50), kind=kLoop, calls=%fused_computation.3 | loop fusion | flops 31457280 | bytes 15341568 | tf_op jit(solution)/shard_map/concatenate | solution.py:76
  6.9 103.4 %all_to_all.21 = bf16[128,40,768]{2,1,0:T(8,128)(2,1)S(1)} all-to-all(bf16[128,40,768]{2,1,0:T(8,128)(2,1)S(1)} %fusion.1), channel_id=1, replica_groups=mesh['rep_hi'=8,'core'=2,'shard'=8] {'shard','rep_hi','core'}, dimensions={0} | all-to-all | bytes 15728640 | tf_op jit(solution)/shard_map/all_to_all | solution.py:78
  110.3 1.1 convert_reduce_fusion
  111.5 0.1 broadcast_in_dim.14
  111.5 18.0 %all_to_all.22 = f32[8,40,768]{2,1,0:T(8,128)S(1)} all-to-all(f32[8,40,768]{2,1,0:T(8,128)S(1)} %broadcast_in_dim.14), channel_id=1, replica_groups=mesh['rep_hi'=8,'core'=2,'shard'=8] {'rep_hi'}, dimensions={0} | all-to-all | bytes 1966080 | tf_op jit(solution)/shard_map/all_to_all | solution.py:32
  129.5 1.6 collective-permute-start
  131.1 0.1 reshape.110
  131.2 0.1 reshape.111
  131.3 0.7 reshape.112
  131.9 1.4 collective-permute-done
  133.3 0.1 select_bitcast_fusion.1
  133.4 1.1 multiply_reduce_fusion
  134.5 0.6 broadcast_in_dim.15
  135.2 10.8 %all_to_all.23 = f32[8,1,1]{2,1,0:T(1,128)S(1)} all-to-all(f32[8,1,1]{2,1,0:T(1,128)S(1)} %broadcast_in_dim.15), channel_id=1, replica_groups=mesh['rep_hi'=8,'core'=2,'shard'=8] {'shard'}, dimensions={0} | all-to-all | bytes 64 | tf_op jit(solution)/shard_map/all_to_all | solution.py:32
  146.0 0.6 reduce_sum.29
  147.4 1.1 subtract_convert_fusion
  148.5 0.9 subtract_convert_fusion.1
  149.4 0.8 convert_bitcast_fusion
  150.2 0.3 broadcast_in_dim.16
  150.5 52.9 %all_to_all.24 = bf16[64,40,768]{2,1,0:T(8,128)(2,1)} all-to-all(bf16[64,40,768]{2,1,0:T(8,128)(2,1)S(1)} %broadcast_in_dim.16), channel_id=1, replica_groups=mesh['rep_hi'=8,'core'=2,'shard'=8] {'shard','rep_hi'}, dimensions={0} | all-to-all | bytes 7864320 | tf_op jit(solution)/shard_map/all_to_all | solution.py:32
  203.4 2.4 %collective-permute-start.1 = (bf16[64,40,768]{2,1,0:T(8,128)(2,1)}, bf16[64,40,768]{2,1,0:T(8,128)(2,1)}, u32[]{:S(2)}, u32[]{:S(2)}) collective-permute-start(bf16[64,40,768]{2,1,0:T(8,128)(2,1)} %all_to_all.24), channel_id=1, source_target_pairs={{0,8},{8,0},{1,9},{9,1},{2,10},{10,2},{3,11},{11,3},{4,12},{12,4},... | collective-permute-start | bytes 11796488 | tf_op jit(solution)/shard_map/ppermute | solution.py:122
  205.8 0.8 slice_multiply_fusion.1
  206.6 1.8 mul.351
  208.4 0.1 mul.367
  208.5 1.3 multiply_subtract_fusion.2
  209.8 2.3 multiply_subtract_fusion.1
  212.1 0.2 slice_multiply_fusion
  212.2 1.2 copy-done.2
  213.5 0.5 copy-done.3
  213.9 3.0 %multiply_subtract_fusion = (f32[512,768]{1,0:T(8,128)}, f32[512,768]{1,0:T(8,128)}, f32[512,768]{1,0:T(8,128)}) fusion(f32[512,768]{1,0:T(8,128)S(1)} %copy-done.1, f32[16,32,768]{2,1,0:T(8,128)S(1)} %slice_multiply_fusion, f32[512,768]{1,0:T(8,128)S(1)} %copy-done.2, f32[512,768]{1,0:T(8,128)S(1)} %copy-done.3), kind=kLoop, calls=%fused_computation.15 | loop fusion | flops 5898240 | bytes 11010048 | tf_op jit(solution)/shard_map/sub | solution.py:26
  216.9 1.3 slice.62
  218.3 2.1 slice_bitcast_fusion.3
  220.3 2.1 slice_bitcast_fusion.1
  222.4 1.3 slice.63
  223.8 0.2 copy.59
  224.1 0.1 select_n.85
  224.1 0.1 reshape_squeeze.16
  224.2 0.7 reshape.114
  224.9 1.3 slice_bitcast_fusion.2
  226.2 0.1 copy-done
  226.3 0.5 maximum_select_fusion.1
  226.8 1.3 copy.58
  228.1 3.2 %select_n.82 = bf16[768,768]{1,0:T(8,128)(2,1)} reshape(bf16[64,2,6,768]{3,2,1,0:T(8,128)(2,1)} %copy.58) | data formatting | bytes 2359296 | tf_op jit(solution)/shard_map/jit(_where)/select_n | solution.py:126
  231.3 2.1 slice_bitcast_fusion
  233.4 3.0 %maximum_select_fusion = bf16[64,2,32,768]{3,2,1,0:T(8,128)(2,1)} fusion(bf16[64,1,32,768]{3,2,1,0:T(8,128)(2,1)S(1)} %slice_bitcast_fusion, bf16[64,1,32,768]{3,2,1,0:T(8,128)(2,1)S(1)} %slice_bitcast_fusion.1, pred[]{:T(512)S(6)} %eq.2), kind=kLoop, calls=%fused_computation.4 | loop fusion | flops 9437184 | bytes 12582913 | tf_op jit(solution)/shard_map/jit(_where)/select_n | solution.py:126
  (24 shorter events, 0.2 us)
Async XLA Ops:
  0.6 2.3 copy-start.8
  111.4 18.1 %copy-start.4 = (f32[40,768]{1,0:T(8,128)}, f32[40,768]{1,0:T(8,128)S(1)}, u32[]{:S(2)}) copy-start(f32[40,768]{1,0:T(8,128)S(1)} %convert_reduce_fusion) | copy-start | bytes 368644
  111.4 19.7 %copy-start.7 = (f32[4,96]{1,0:T(4,128)S(1)}, f32[4,96]{1,0:T(4,128)}, u32[]{:S(2)}) copy-start(f32[4,96]{1,0:T(4,128)} %param.21) | copy-start | bytes 4612
  111.4 19.7 %copy-start.6 = (f32[4,96]{1,0:T(4,128)S(1)}, f32[4,96]{1,0:T(4,128)}, u32[]{:S(2)}) copy-start(f32[4,96]{1,0:T(4,128)} %param.22) | copy-start | bytes 4612
  111.4 19.8 %copy-start.5 = (f32[4,96]{1,0:T(4,128)S(1)}, f32[4,96]{1,0:T(4,128)}, u32[]{:S(2)}) copy-start(f32[4,96]{1,0:T(4,128)} %param.23) | copy-start | bytes 4612
  129.5 3.8 %collective-permute-start = (f32[8,40,768]{2,1,0:T(8,128)S(1)}, f32[8,40,768]{2,1,0:T(8,128)S(1)}, u32[]{:S(2)}, u32[]{:S(2)}) collective-permute-start(f32[8,40,768]{2,1,0:T(8,128)S(1)} %all_to_all.22), channel_id=1, source_target_pairs={{0,8},{8,0},{1,9},{9,1},{2,10},{10,2},{3,11},{11,3},{4,12},{12,4},... | collective-permute-start | bytes 2949128 | tf_op jit(solution)/shard_map/ppermute | solution.py:82
  133.4 14.0 %copy-start.1 = (f32[512,768]{1,0:T(8,128)S(1)}, f32[512,768]{1,0:T(8,128)}, u32[]{:S(2)}) copy-start(f32[512,768]{1,0:T(8,128)} %param.15) | copy-start | bytes 4718596
  203.4 19.0 %collective-permute-start.1 = (bf16[64,40,768]{2,1,0:T(8,128)(2,1)}, bf16[64,40,768]{2,1,0:T(8,128)(2,1)}, u32[]{:S(2)}, u32[]{:S(2)}) collective-permute-start(bf16[64,40,768]{2,1,0:T(8,128)(2,1)} %all_to_all.24), channel_id=1, source_target_pairs={{0,8},{8,0},{1,9},{9,1},{2,10},{10,2},{3,11},{11,3},{4,12},{12,4},... | collective-permute-start | bytes 11796488 | tf_op jit(solution)/shard_map/ppermute | solution.py:122
  212.1 1.4 copy-start.2
  212.1 1.9 copy-start.3
  224.9 1.4 copy-start

commit v3 on v0

--- a/solution.py
+++ b/solution.py
@@ -87,8 +87,8 @@
     embed_sum = block[:, :e_rows].reshape(n_rep * e_rows, width)
     proj_sum = block[:, e_rows : e_rows + p_rows].reshape(n_rep * p_rows, width)
     norm_sum = block[:, e_rows + p_rows, :n_vals].reshape(norm_rows, block_norm)
-    partial = jnp.sum(block * block)
-    squares = jnp.sum(gather_all(partial.reshape(1), "shard"))
+    partial = jnp.sum(half_block * half_block)
+    squares = jnp.sum(gather_all(partial.reshape(1), ("shard", "core")))
     rms_value = jnp.sqrt(squares / entry_count)
     clip_factor = jnp.minimum(jnp.float32(1.0), clip_rms / (rms_value + 1e-06))
 

time: 230 us -> 229 us (level)
  blocking collectives: 185 us -> 175 us
  waiting for transfers between devices: 1.36 us -> 9.01 us
  starting transfers between devices: 3.99 us -> 8.33 us
    all_to_all x3 -> x2, blocking collectives: 81.8 us -> 71.9 us  [gather_all(): lax.all_to_all(jnp.broadcast_to(piece[None], (count,) + piece.shape), axi...]
    all_to_all x0 -> x1, waiting for transfers between devices: none -> 6.94 us  [gather_all(): lax.all_to_all(jnp.broadcast_to(piece[None], (count,) + piece.shape), axi...]
    all_to_all x0 -> x1, starting transfers between devices: none -> 5.16 us  [gather_all(): lax.all_to_all(jnp.broadcast_to(piece[None], (count,) + piece.shape), axi...]
    another operation x1 -> x2, other arithmetic: 0.14 us -> 3.08 us  [shards(): jnp.stack([jnp.where(core == 0, half_block, half_other), jnp.where(core =...]
  transfers between devices with their start and end apart: 2 -> 3, of which waited for: 1 -> 2; matrix products, arithmetic and copies ran while one was open for 4% -> 2% of each run, Pallas kernels for 0% -> 0%
where the time goes in v3:
time: 229 us
  blocking collectives  175 us (76%)
  other arithmetic  25.7 us (11%)
  waiting for transfers between devices  9.01 us (4%)
  local copies, waits for them, and re-layouts  8.81 us (4%)
  starting transfers between devices  8.33 us (4%)
    all_to_all x1, blocking collectives, shards(): received = lax.all_to_all(send, ALL, 0, 0, tiled=True)  103 us
    all_to_all x2, blocking collectives, gather_all(): lax.all_to_all(jnp.broadcast_to(piece[None], (count,) + piece.shape), axi...  71.9 us
    another operation x5, other arithmetic, interleave(): return jnp.stack(pair, axis=1).reshape((n_all, hi - lo) + w_piece.shape[1:])  8.22 us
    all_to_all x1, waiting for transfers between devices, gather_all(): lax.all_to_all(jnp.broadcast_to(piece[None], (count,) + piece.shape), axi...  6.94 us
    all_to_all x1, starting transfers between devices, gather_all(): lax.all_to_all(jnp.broadcast_to(piece[None], (count,) + piece.shape), axi...  5.16 us
    sub x3, other arithmetic, adamw(): master_new = master - learning_rate * direction  4.63 us
  transfers between devices with their start and end apart: 3, of which 2 were waited for; matrix products, arithmetic and copies ran while one was open for 2% of the time, Pallas kernels for 0%

profile of v3, /device:TPU:1, one launch (start us, length us, event | category | flops | bytes accessed | tf_op | source)
XLA Modules:
  0.0 228.8 jit_solution(12581585504972669969)
XLA Ops:
  0.7 2.2 reshape_squeeze.14
  2.9 0.1 reshape_squeeze.15
  3.0 0.1 reshape.74
  3.1 3.8 %fusion.1 = bf16[128,40,768]{2,1,0:T(8,128)(2,1)S(1)} fusion(bf16[128,1,24]{2,1,0:T(2,128)(2,1)S(1)} %reshape.74, bf16[128,6,768]{2,1,0:T(8,128)(2,1)S(1)} %reshape_squeeze.14, bf16[128,32,768]{2,1,0:T(8,128)(2,1)} %bitcast.50), kind=kLoop, calls=%fused_computation.3 | loop fusion | flops 31457280 | bytes 15341568 | tf_op jit(solution)/shard_map/concatenate | solution.py:76
  6.9 103.4 %all_to_all.21 = bf16[128,40,768]{2,1,0:T(8,128)(2,1)S(1)} all-to-all(bf16[128,40,768]{2,1,0:T(8,128)(2,1)S(1)} %fusion.1), channel_id=1, replica_groups=mesh['rep_hi'=8,'core'=2,'shard'=8] {'shard','rep_hi','core'}, dimensions={0} | all-to-all | bytes 15728640 | tf_op jit(solution)/shard_map/all_to_all | solution.py:78
  110.3 1.1 convert_reduce_fusion
  111.4 0.0 copy-start.8
  111.4 0.1 broadcast_in_dim.6
  111.5 18.0 %all_to_all.22 = f32[8,40,768]{2,1,0:T(8,128)S(1)} all-to-all(f32[8,40,768]{2,1,0:T(8,128)S(1)} %broadcast_in_dim.6), channel_id=1, replica_groups=mesh['rep_hi'=8,'core'=2,'shard'=8] {'rep_hi'}, dimensions={0} | all-to-all | bytes 1966080 | tf_op jit(solution)/shard_map/all_to_all | solution.py:32
  129.5 1.6 collective-permute-start
  131.1 0.1 reshape.68
  131.2 0.1 reshape.69
  131.2 0.1 reshape.70
  131.3 2.1 collective-permute-done
  133.4 2.9 %select_bitcast_fusion.3 = (f32[8,1,40,768]{3,2,1,0:T(8,128)S(1)}, f32[8,1,40,768]{3,2,1,0:T(8,128)}, f32[]{:T(128)}) fusion(f32[8,40,768]{2,1,0:T(8,128)S(1)} %all_to_all.22, f32[8,40,768]{2,1,0:T(8,128)} %collective-permute-done, pred[]{:T(512)S(6)} %eq.2), kind=kLoop, calls=%fused_computation.16 | loop fusion | flops 983039 | bytes 3932165 | tf_op jit(solution)/shard_map/stack | solution.py:83
  136.3 1.2 broadcast_in_dim.7
  137.6 5.2 %all-to-all-start.2 = ((f32[16,1,1]{2,1,0:T(1,128)}), f32[16,1,1]{2,1,0:T(1,128)S(1)}, u32[]{:S(2)}, u32[]{:S(2)}) async-start(f32[16,1,1]{2,1,0:T(1,128)} %broadcast_in_dim.7), calls=%async_computation.2 | async-start | bytes 16384 | tf_op jit(solution)/shard_map/all_to_all | solution.py:32
  142.7 6.9 %all-to-all-done.2 = f32[16,1,1]{2,1,0:T(1,128)S(1)} async-done(((f32[16,1,1]{2,1,0:T(1,128)}), f32[16,1,1]{2,1,0:T(1,128)S(1)}, u32[]{:S(2)}, u32[]{:S(2)}) %all-to-all-start.2) | async-done | bytes 96 | tf_op jit(solution)/shard_map/all_to_all | solution.py:32
  149.7 0.6 reduce_sum.29
  151.0 1.1 subtract_convert_fusion
  152.1 0.9 subtract_convert_fusion.1
  153.0 0.1 convert_bitcast_fusion
  153.1 0.3 broadcast_in_dim.8
  153.4 0.0 copy-start
  153.4 53.9 %all_to_all.23 = bf16[64,40,768]{2,1,0:T(8,128)(2,1)} all-to-all(bf16[64,40,768]{2,1,0:T(8,128)(2,1)S(1)} %broadcast_in_dim.8), channel_id=1, replica_groups=mesh['rep_hi'=8,'core'=2,'shard'=8] {'shard','rep_hi'}, dimensions={0} | all-to-all | bytes 7864320 | tf_op jit(solution)/shard_map/all_to_all | solution.py:32
  207.3 1.6 collective-permute-start.1
  208.9 0.1 pad_maximum_fusion.1
  209.1 0.0 copy-start.6
  209.2 0.1 mul.366
  209.3 0.6 multiply_subtract_fusion.2
  209.9 0.1 copy-done.6
  210.0 1.0 multiply_subtract_fusion.1
  211.1 0.2 slice_multiply_fusion
  211.2 0.5 copy-done.3
  211.8 0.8 copy-done.1
  212.6 0.5 copy-done.2
  213.1 3.0 %multiply_subtract_fusion = (f32[512,768]{1,0:T(8,128)}, f32[512,768]{1,0:T(8,128)}, f32[512,768]{1,0:T(8,128)}) fusion(f32[512,768]{1,0:T(8,128)S(1)} %copy-done.1, f32[16,32,768]{2,1,0:T(8,128)S(1)} %slice_multiply_fusion, f32[512,768]{1,0:T(8,128)S(1)} %copy-done.2, f32[512,768]{1,0:T(8,128)S(1)} %copy-done.3), kind=kLoop, calls=%fused_computation.14 | loop fusion | flops 5898240 | bytes 11010048 | tf_op jit(solution)/shard_map/sub | solution.py:26
  216.1 2.0 broadcast_select_fusion.1
  218.1 0.2 copy.67
  218.3 0.1 reshape.72
  218.4 0.1 reshape_squeeze.16
  218.5 0.7 reshape.73
  219.2 1.5 select_bitcast_fusion.5
  220.7 0.4 pad_maximum_fusion.2
  221.1 0.1 copy.66
  221.2 1.2 reshape_reshape.7
  222.4 3.1 %select_bitcast_fusion.1 = (bf16[64,1,32,768]{3,2,1,0:T(8,128)(2,1)S(1)}, bf16[64,1,32,768]{3,2,1,0:T(8,128)(2,1)S(1)}) fusion(pred[]{:T(512)S(6)} %eq.2, bf16[64,40,768]{2,1,0:T(8,128)(2,1)} %collective-permute-done.1, bf16[64,40,768]{2,1,0:T(8,128)(2,1)} %all_to_all.23), kind=kLoop, calls=%fused_computation.6 | loop fusion | flops 3145728 | bytes 12582913 | tf_op jit(solution)/shard_map/stack | solution.py:127
  225.5 3.3 %pad_maximum_fusion = bf16[64,2,32,768]{3,2,1,0:T(8,128)(2,1)} fusion(bf16[64,1,32,768]{3,2,1,0:T(8,128)(2,1)S(1)} %get-tuple-element.26, bf16[64,1,32,768]{3,2,1,0:T(8,128)(2,1)S(1)} %get-tuple-element.25), kind=kLoop, calls=%fused_computation.4 | loop fusion | flops 3145728 | bytes 12582912 | tf_op jit(solution)/shard_map/stack | solution.py:127
  (25 shorter events, 0.2 us)
Async XLA Ops:
  0.6 2.3 copy-start.10
  111.4 19.7 %copy-start.9 = (f32[4,96]{1,0:T(4,128)S(1)}, f32[4,96]{1,0:T(4,128)}, u32[]{:S(2)}) copy-start(f32[4,96]{1,0:T(4,128)} %param.21) | copy-start | bytes 4612
  111.4 19.7 %copy-start.8 = (f32[4,96]{1,0:T(4,128)S(1)}, f32[4,96]{1,0:T(4,128)}, u32[]{:S(2)}) copy-start(f32[4,96]{1,0:T(4,128)} %param.22) | copy-start | bytes 4612
  111.4 19.8 %copy-start.7 = (f32[4,96]{1,0:T(4,128)S(1)}, f32[4,96]{1,0:T(4,128)}, u32[]{:S(2)}) copy-start(f32[4,96]{1,0:T(4,128)} %param.23) | copy-start | bytes 4612
  129.5 3.9 %collective-permute-start = (f32[8,40,768]{2,1,0:T(8,128)S(1)}, f32[8,40,768]{2,1,0:T(8,128)}, u32[]{:S(2)}, u32[]{:S(2)}) collective-permute-start(f32[8,40,768]{2,1,0:T(8,128)S(1)} %all_to_all.22), channel_id=1, source_target_pairs={{0,8},{8,0},{1,9},{9,1},{2,10},{10,2},{3,11},{11,3},{4,12},{12,4},... | collective-permute-start | bytes 2949128 | tf_op jit(solution)/shard_map/ppermute | solution.py:82
  131.3 20.8 %copy-start.4 = (f32[96,768]{1,0:T(8,128)S(1)}, f32[96,768]{1,0:T(8,128)}, u32[]{:S(2)}) copy-start(f32[96,768]{1,0:T(8,128)} %param.20) | copy-start | bytes 884740
  131.3 20.8 %copy-start.5 = (f32[96,768]{1,0:T(8,128)S(1)}, f32[96,768]{1,0:T(8,128)}, u32[]{:S(2)}) copy-start(f32[96,768]{1,0:T(8,128)} %param.19) | copy-start | bytes 884740
  137.6 12.1 %all-to-all-start.2 = ((f32[16,1,1]{2,1,0:T(1,128)}), f32[16,1,1]{2,1,0:T(1,128)S(1)}, u32[]{:S(2)}, u32[]{:S(2)}) async-start(f32[16,1,1]{2,1,0:T(1,128)} %broadcast_in_dim.7), calls=%async_computation.2 | async-start | bytes 16384 | tf_op jit(solution)/shard_map/all_to_all | solution.py:32
  153.4 55.5 %copy-start = (f32[8,1,40,768]{3,2,1,0:T(8,128)S(1)}, f32[8,1,40,768]{3,2,1,0:T(8,128)}, u32[]{:S(2)}) copy-start(f32[8,1,40,768]{3,2,1,0:T(8,128)} %get-tuple-element.28) | copy-start | bytes 2949124
  207.3 8.8 %collective-permute-start.1 = (bf16[64,40,768]{2,1,0:T(8,128)(2,1)}, bf16[64,40,768]{2,1,0:T(8,128)(2,1)}, u32[]{:S(2)}, u32[]{:S(2)}) collective-permute-start(bf16[64,40,768]{2,1,0:T(8,128)(2,1)} %all_to_all.23), channel_id=1, source_target_pairs={{0,8},{8,0},{1,9},{9,1},{2,10},{10,2},{3,11},{11,3},{4,12},{12,4},... | collective-permute-start | bytes 11796488 | tf_op jit(solution)/shard_map/ppermute | solution.py:122
  209.1 1.0 copy-start.6
  210.0 1.7 copy-start.3
  211.1 1.5 copy-start.1
  211.1 2.0 copy-start.2

commit v4 on v3

--- a/solution.py
+++ b/solution.py
@@ -80,17 +80,18 @@
 
     half_block = gather_all(reduced, "rep_hi")
     half_other = lax.ppermute(half_block, "core", [(0, 1), (1, 0)])
+    partial = jnp.sum(half_block * half_block)
+    squares = jnp.sum(gather_all(partial.reshape(1), ("shard", "core")))
+    rms_value = jnp.sqrt(squares / entry_count)
+    clip_factor = jnp.minimum(jnp.float32(1.0), clip_rms / (rms_value + 1e-06))
+    half_mine, half_other, _ = lax.optimization_barrier((half_block, half_other, clip_factor))
     block = jnp.stack(
-        [jnp.where(core == 0, half_block, half_other), jnp.where(core == 0, half_other, half_block)],
+        [jnp.where(core == 0, half_mine, half_other), jnp.where(core == 0, half_other, half_mine)],
         axis=1,
     ).reshape((n_rep,) + reduced.shape)
     embed_sum = block[:, :e_rows].reshape(n_rep * e_rows, width)
     proj_sum = block[:, e_rows : e_rows + p_rows].reshape(n_rep * p_rows, width)
     norm_sum = block[:, e_rows + p_rows, :n_vals].reshape(norm_rows, block_norm)
-    partial = jnp.sum(half_block * half_block)
-    squares = jnp.sum(gather_all(partial.reshape(1), ("shard", "core")))
-    rms_value = jnp.sqrt(squares / entry_count)
-    clip_factor = jnp.minimum(jnp.float32(1.0), clip_rms / (rms_value + 1e-06))
 
     def flat_norm(x):
         return lax.dynamic_slice(x.reshape(-1), (rep_index * n_vals,), (n_vals,))

time: 229 us -> 238 us (1.039)
  waiting for transfers between devices: 9.01 us -> 29.9 us
  blocking collectives: 175 us -> 157 us
  starting transfers between devices: 8.33 us -> 11.1 us
  local copies, waits for them, and re-layouts: 8.81 us -> 11.2 us
    all_to_all x2 -> x1, blocking collectives: 71.9 us -> 53.8 us  [gather_all(): lax.all_to_all(jnp.broadcast_to(piece[None], (count,) + piece.shape), axi...]
    all_to_all x1 -> x2, waiting for transfers between devices: 6.94 us -> 21.8 us  [gather_all(): lax.all_to_all(jnp.broadcast_to(piece[None], (count,) + piece.shape), axi...]
    ppermute x1, waiting for transfers between devices: 2.06 us -> 8.02 us  [shards(): half_other = lax.ppermute(half_block, 'core', [(0, 1), (1, 0)])]
    all_to_all x1 -> x2, starting transfers between devices: 5.16 us -> 9.51 us  [gather_all(): lax.all_to_all(jnp.broadcast_to(piece[None], (count,) + piece.shape), axi...]
    another operation x2, other arithmetic: 3.08 us -> 0.28 us  [shards(): jnp.stack([jnp.where(core == 0, half_mine, half_other), jnp.where(core ==...]
  transfers between devices with their start and end apart: 3 -> 4, of which waited for: 2 -> 3; matrix products, arithmetic and copies ran while one was open for 2% -> 4% of each run, Pallas kernels for 0% -> 0%
where the time goes in v4:
time: 238 us; the launch traced here: 237 us
  blocking collectives  157 us (66%)
  waiting for transfers between devices  29.9 us (13%)
  other arithmetic  26.4 us (11%)
  local copies, waits for them, and re-layouts  11.2 us (5%)
  starting transfers between devices  11.1 us (5%)
    all_to_all x1, blocking collectives, shards(): received = lax.all_to_all(send, ALL, 0, 0, tiled=True)  103 us
    all_to_all x1, blocking collectives, gather_all(): lax.all_to_all(jnp.broadcast_to(piece[None], (count,) + piece.shape), axi...  53.8 us
    all_to_all x2, waiting for transfers between devices, gather_all(): lax.all_to_all(jnp.broadcast_to(piece[None], (count,) + piece.shape), axi...  21.8 us
    all_to_all x2, starting transfers between devices, gather_all(): lax.all_to_all(jnp.broadcast_to(piece[None], (count,) + piece.shape), axi...  9.51 us
    another operation x5, other arithmetic, interleave(): return jnp.stack(pair, axis=1).reshape((n_all, hi - lo) + w_piece.shape[1:])  8.22 us
    ppermute x1, waiting for transfers between devices, shards(): half_other = lax.ppermute(half_block, 'core', [(0, 1), (1, 0)])  8.02 us
    sub x3, other arithmetic, adamw(): master_new = master - learning_rate * direction  6.54 us
  transfers between devices with their start and end apart: 4, of which 3 were waited for; matrix products, arithmetic and copies ran while one was open for 4% of the time, Pallas kernels for 0%

profile of v4, /device:TPU:1, one launch (start us, length us, event | category | flops | bytes accessed | tf_op | source)
XLA Modules:
  0.0 237.4 jit_solution(15357946449240915494)
XLA Ops:
  0.7 2.2 reshape_squeeze.14
  2.9 0.1 reshape_squeeze.15
  3.0 0.1 reshape.74
  3.1 3.8 %fusion.1 = bf16[128,40,768]{2,1,0:T(8,128)(2,1)S(1)} fusion(bf16[128,1,24]{2,1,0:T(2,128)(2,1)S(1)} %reshape.74, bf16[128,6,768]{2,1,0:T(8,128)(2,1)S(1)} %reshape_squeeze.14, bf16[128,32,768]{2,1,0:T(8,128)(2,1)} %bitcast.50), kind=kLoop, calls=%fused_computation.3 | loop fusion | flops 31457280 | bytes 15341568 | tf_op jit(solution)/shard_map/concatenate | solution.py:76
  6.9 103.4 %all_to_all.21 = bf16[128,40,768]{2,1,0:T(8,128)(2,1)S(1)} all-to-all(bf16[128,40,768]{2,1,0:T(8,128)(2,1)S(1)} %fusion.1), channel_id=1, replica_groups=mesh['rep_hi'=8,'core'=2,'shard'=8] {'shard','rep_hi','core'}, dimensions={0} | all-to-all | bytes 15728640 | tf_op jit(solution)/shard_map/all_to_all | solution.py:78
  110.3 1.1 convert_reduce_fusion
  111.4 0.0 copy-start.4
  111.4 0.0 copy-start.3
  111.4 1.0 broadcast_in_dim.6
  112.5 3.9 %all-to-all-start.1 = ((f32[8,40,768]{2,1,0:T(8,128)}), f32[8,40,768]{2,1,0:T(8,128)S(1)}, u32[]{:S(2)}, u32[]{:S(2)}) async-start(f32[8,40,768]{2,1,0:T(8,128)} %broadcast_in_dim.6), calls=%async_computation.1 | async-start | bytes 1966080 | tf_op jit(solution)/shard_map/all_to_all | solution.py:32
  116.4 0.1 reshape.68
  116.5 0.1 reshape.69
  116.6 0.1 reshape.70
  116.6 14.9 %all-to-all-done.1 = f32[8,40,768]{2,1,0:T(8,128)S(1)} async-done(((f32[8,40,768]{2,1,0:T(8,128)}), f32[8,40,768]{2,1,0:T(8,128)S(1)}, u32[]{:S(2)}, u32[]{:S(2)}) %all-to-all-start.1) | async-done | bytes 983072 | tf_op jit(solution)/shard_map/all_to_all | solution.py:32
  131.6 0.8 multiply_reduce_fusion
  132.4 1.2 broadcast_in_dim.7
  133.6 5.6 %all-to-all-start.2 = ((f32[16,1,1]{2,1,0:T(1,128)}), f32[16,1,1]{2,1,0:T(1,128)S(1)}, u32[]{:S(2)}, u32[]{:S(2)}) async-start(f32[16,1,1]{2,1,0:T(1,128)} %broadcast_in_dim.7), calls=%async_computation.2 | async-start | bytes 16384 | tf_op jit(solution)/shard_map/all_to_all | solution.py:32
  139.2 6.9 %all-to-all-done.2 = f32[16,1,1]{2,1,0:T(1,128)S(1)} async-done(((f32[16,1,1]{2,1,0:T(1,128)}), f32[16,1,1]{2,1,0:T(1,128)S(1)}, u32[]{:S(2)}, u32[]{:S(2)}) %all-to-all-start.2) | async-done | bytes 96 | tf_op jit(solution)/shard_map/all_to_all | solution.py:32
  146.2 0.6 reduce_sum.29
  147.5 1.0 subtract_convert_fusion
  148.6 0.9 subtract_convert_fusion.1
  149.5 0.1 convert_bitcast_fusion
  149.6 0.3 broadcast_in_dim.8
  149.8 53.8 %all_to_all.22 = bf16[64,40,768]{2,1,0:T(8,128)(2,1)} all-to-all(bf16[64,40,768]{2,1,0:T(8,128)(2,1)S(1)} %broadcast_in_dim.8), channel_id=1, replica_groups=mesh['rep_hi'=8,'core'=2,'shard'=8] {'shard','rep_hi'}, dimensions={0} | all-to-all | bytes 7864320 | tf_op jit(solution)/shard_map/all_to_all | solution.py:32
  203.6 1.6 collective-permute-start.1
  205.2 8.0 %collective-permute-done = f32[8,40,768]{2,1,0:T(8,128)S(1)} collective-permute-done((f32[8,40,768]{2,1,0:T(8,128)S(1)}, f32[8,40,768]{2,1,0:T(8,128)S(1)}, u32[]{:S(2)}, u32[]{:S(2)}) %collective-permute-start) | collective-permute-done | bytes 983072 | tf_op jit(solution)/shard_map/ppermute | solution.py:82
  213.3 0.1 select_bitcast_fusion.3
  213.4 0.1 pad_maximum_fusion.1
  213.6 0.8 slice_multiply_fusion.1
  214.3 1.8 mul.350
  216.1 0.1 mul.366
  216.2 1.3 multiply_subtract_fusion.2
  217.5 2.3 multiply_subtract_fusion.1
  219.8 0.2 slice_multiply_fusion
  220.0 1.2 copy-done.1
  221.2 0.5 copy-done.2
  221.7 3.0 %multiply_subtract_fusion = (f32[512,768]{1,0:T(8,128)}, f32[512,768]{1,0:T(8,128)}, f32[512,768]{1,0:T(8,128)}) fusion(f32[512,768]{1,0:T(8,128)S(1)} %copy-done, f32[16,32,768]{2,1,0:T(8,128)S(1)} %slice_multiply_fusion, f32[512,768]{1,0:T(8,128)S(1)} %copy-done.1, f32[512,768]{1,0:T(8,128)S(1)} %copy-done.2), kind=kLoop, calls=%fused_computation.14 | loop fusion | flops 5898240 | bytes 11010048 | tf_op jit(solution)/shard_map/sub | solution.py:26
  224.6 2.0 broadcast_select_fusion.1
  226.7 0.2 copy.67
  226.9 0.1 reshape.72
  227.0 0.1 reshape_squeeze.16
  227.1 0.7 reshape.73
  227.8 1.5 select_bitcast_fusion.5
  229.3 0.4 pad_maximum_fusion.2
  229.6 0.1 copy.66
  229.7 1.2 reshape_reshape.7
  231.0 3.1 %select_bitcast_fusion.1 = (bf16[64,1,32,768]{3,2,1,0:T(8,128)(2,1)S(1)}, bf16[64,1,32,768]{3,2,1,0:T(8,128)(2,1)S(1)}) fusion(pred[]{:T(512)S(6)} %eq.2, bf16[64,40,768]{2,1,0:T(8,128)(2,1)} %collective-permute-done.1, bf16[64,40,768]{2,1,0:T(8,128)(2,1)} %all_to_all.22), kind=kLoop, calls=%fused_computation.6 | loop fusion | flops 3145728 | bytes 12582913 | tf_op jit(solution)/shard_map/stack | solution.py:128
  234.1 3.3 %pad_maximum_fusion = bf16[64,2,32,768]{3,2,1,0:T(8,128)(2,1)} fusion(bf16[64,1,32,768]{3,2,1,0:T(8,128)(2,1)S(1)} %get-tuple-element.30, bf16[64,1,32,768]{3,2,1,0:T(8,128)(2,1)S(1)} %get-tuple-element.29), kind=kLoop, calls=%fused_computation.4 | loop fusion | flops 3145728 | bytes 12582912 | tf_op jit(solution)/shard_map/stack | solution.py:128
  (19 shorter events, 0.1 us)
Async XLA Ops:
  0.6 2.3 copy-start.6
  111.4 5.0 %copy-start.5 = (f32[4,96]{1,0:T(4,128)S(1)}, f32[4,96]{1,0:T(4,128)}, u32[]{:S(2)}) copy-start(f32[4,96]{1,0:T(4,128)} %param.21) | copy-start | bytes 4612
  111.4 5.1 %copy-start.4 = (f32[4,96]{1,0:T(4,128)S(1)}, f32[4,96]{1,0:T(4,128)}, u32[]{:S(2)}) copy-start(f32[4,96]{1,0:T(4,128)} %param.22) | copy-start | bytes 4612
  111.4 5.1 %copy-start.3 = (f32[4,96]{1,0:T(4,128)S(1)}, f32[4,96]{1,0:T(4,128)}, u32[]{:S(2)}) copy-start(f32[4,96]{1,0:T(4,128)} %param.23) | copy-start | bytes 4612
  112.5 35.1 %copy-start = (f32[512,768]{1,0:T(8,128)S(1)}, f32[512,768]{1,0:T(8,128)}, u32[]{:S(2)}) copy-start(f32[512,768]{1,0:T(8,128)} %param.15) | copy-start | bytes 4718596
  112.5 19.1 %all-to-all-start.1 = ((f32[8,40,768]{2,1,0:T(8,128)}), f32[8,40,768]{2,1,0:T(8,128)S(1)}, u32[]{:S(2)}, u32[]{:S(2)}) async-start(f32[8,40,768]{2,1,0:T(8,128)} %broadcast_in_dim.6), calls=%async_computation.1 | async-start | bytes 1966080 | tf_op jit(solution)/shard_map/all_to_all | solution.py:32
  133.6 12.5 %all-to-all-start.2 = ((f32[16,1,1]{2,1,0:T(1,128)}), f32[16,1,1]{2,1,0:T(1,128)S(1)}, u32[]{:S(2)}, u32[]{:S(2)}) async-start(f32[16,1,1]{2,1,0:T(1,128)} %broadcast_in_dim.7), calls=%async_computation.2 | async-start | bytes 16384 | tf_op jit(solution)/shard_map/all_to_all | solution.py:32
  203.6 21.0 %collective-permute-start.1 = (bf16[64,40,768]{2,1,0:T(8,128)(2,1)}, bf16[64,40,768]{2,1,0:T(8,128)(2,1)}, u32[]{:S(2)}, u32[]{:S(2)}) collective-permute-start(bf16[64,40,768]{2,1,0:T(8,128)(2,1)} %all_to_all.22), channel_id=1, source_target_pairs={{0,8},{8,0},{1,9},{9,1},{2,10},{10,2},{3,11},{11,3},{4,12},{12,4},... | collective-permute-start | bytes 11796488 | tf_op jit(solution)/shard_map/ppermute | solution.py:123
  205.2 8.0 %collective-permute-start = (f32[8,40,768]{2,1,0:T(8,128)S(1)}, f32[8,40,768]{2,1,0:T(8,128)S(1)}, u32[]{:S(2)}, u32[]{:S(2)}) collective-permute-start(f32[8,40,768]{2,1,0:T(8,128)S(1)} %all-to-all-done.1), channel_id=1, source_target_pairs={{0,8},{8,0},{1,9},{9,1},{2,10},{10,2},{3,11},{11,3},{4,12},{12,4},... | collective-permute-start | bytes 2949128 | tf_op jit(solution)/shard_map/ppermute | solution.py:82
  219.8 1.4 copy-start.1
  219.8 1.9 copy-start.2

commit v5 on v0

--- a/solution.py
+++ b/solution.py
@@ -80,14 +80,18 @@
 
     half_block = gather_all(reduced, "rep_hi")
     half_other = lax.ppermute(half_block, "core", [(0, 1), (1, 0)])
-    block = jnp.stack(
-        [jnp.where(core == 0, half_block, half_other), jnp.where(core == 0, half_other, half_block)],
-        axis=1,
-    ).reshape((n_rep,) + reduced.shape)
-    embed_sum = block[:, :e_rows].reshape(n_rep * e_rows, width)
-    proj_sum = block[:, e_rows : e_rows + p_rows].reshape(n_rep * p_rows, width)
-    norm_sum = block[:, e_rows + p_rows, :n_vals].reshape(norm_rows, block_norm)
-    partial = jnp.sum(block * block)
+
+    def block_rows(lo, hi):
+        mine, other = half_block[:, lo:hi], half_other[:, lo:hi]
+        pair = [jnp.where(core == 0, mine, other), jnp.where(core == 0, other, mine)]
+        return jnp.stack(pair, axis=1).reshape((n_rep, hi - lo) + reduced.shape[1:])
+
+    embed_sum = block_rows(0, e_rows).reshape(n_rep * e_rows, width)
+    proj_sum = block_rows(e_rows, e_rows + p_rows).reshape(n_rep * p_rows, width)
+    norm_sum = block_rows(e_rows + p_rows, e_rows + p_rows + 1)[:, 0, :n_vals].reshape(
+        norm_rows, block_norm
+    )
+    partial = jnp.sum(half_block * half_block) + jnp.sum(half_other * half_other)
     squares = jnp.sum(gather_all(partial.reshape(1), "shard"))
     rms_value = jnp.sqrt(squares / entry_count)
     clip_factor = jnp.minimum(jnp.float32(1.0), clip_rms / (rms_value + 1e-06))

time: 230 us -> 228 us (level)
  local copies, waits for them, and re-layouts: 10.2 us -> 7.41 us
where the time goes in v5:
time: 228 us
  blocking collectives  185 us (81%)
  other arithmetic  27.1 us (12%)
  local copies, waits for them, and re-layouts  7.41 us (3%)
  starting transfers between devices  3.99 us (2%)
  between operations  2.95 us (1%)
    all_to_all x1, blocking collectives, shards(): received = lax.all_to_all(send, ALL, 0, 0, tiled=True)  103 us
    all_to_all x3, blocking collectives, gather_all(): lax.all_to_all(jnp.broadcast_to(piece[None], (count,) + piece.shape), axi...  81.8 us
    another operation x5, other arithmetic, interleave(): return jnp.stack(pair, axis=1).reshape((n_all, hi - lo) + w_piece.shape[1:])  8.22 us
    sub x3, other arithmetic, adamw(): master_new = master - learning_rate * direction  4.63 us
  transfers between devices with their start and end apart: 2, of which 1 were waited for; matrix products, arithmetic and copies ran while one was open for 4% of the time, Pallas kernels for 0%

profile of v5, /device:TPU:1, one launch (start us, length us, event | category | flops | bytes accessed | tf_op | source)
XLA Modules:
  0.0 227.7 jit_solution(5253300420890305177)
XLA Ops:
  0.7 2.2 reshape_squeeze.14
  2.9 0.1 reshape_squeeze.15
  3.0 0.1 reshape.72
  3.1 3.8 %fusion.1 = bf16[128,40,768]{2,1,0:T(8,128)(2,1)S(1)} fusion(bf16[128,1,24]{2,1,0:T(2,128)(2,1)S(1)} %reshape.72, bf16[128,6,768]{2,1,0:T(8,128)(2,1)S(1)} %reshape_squeeze.14, bf16[128,32,768]{2,1,0:T(8,128)(2,1)} %bitcast.58), kind=kLoop, calls=%fused_computation.3 | loop fusion | flops 31457280 | bytes 15341568 | tf_op jit(solution)/shard_map/concatenate | solution.py:76
  6.9 103.4 %all_to_all.21 = bf16[128,40,768]{2,1,0:T(8,128)(2,1)S(1)} all-to-all(bf16[128,40,768]{2,1,0:T(8,128)(2,1)S(1)} %fusion.1), channel_id=1, replica_groups=mesh['rep_hi'=8,'core'=2,'shard'=8] {'shard','rep_hi','core'}, dimensions={0} | all-to-all | bytes 15728640 | tf_op jit(solution)/shard_map/all_to_all | solution.py:78
  110.3 1.1 convert_reduce_fusion
  111.4 0.1 broadcast_in_dim.6
  111.5 18.0 %all_to_all.22 = f32[8,40,768]{2,1,0:T(8,128)S(1)} all-to-all(f32[8,40,768]{2,1,0:T(8,128)S(1)} %broadcast_in_dim.6), channel_id=1, replica_groups=mesh['rep_hi'=8,'core'=2,'shard'=8] {'rep_hi'}, dimensions={0} | all-to-all | bytes 1966080 | tf_op jit(solution)/shard_map/all_to_all | solution.py:32
  129.5 1.6 collective-permute-start
  131.1 0.1 reshape.65
  131.2 0.1 reshape.66
  131.2 0.1 reshape.67
  131.3 0.9 multiply_reduce_fusion.1
  132.2 1.1 collective-permute-done
  133.3 0.8 multiply_reduce_fusion
  135.4 10.8 %all_to_all.23 = f32[8,1,1]{2,1,0:T(1,128)S(1)} all-to-all(f32[8,1,1]{2,1,0:T(1,128)S(1)} %broadcast_in_dim.7), channel_id=1, replica_groups=mesh['rep_hi'=8,'core'=2,'shard'=8] {'shard'}, dimensions={0} | all-to-all | bytes 64 | tf_op jit(solution)/shard_map/all_to_all | solution.py:32
  146.3 0.6 reduce_sum.39
  147.6 1.1 subtract_convert_fusion
  148.7 0.9 subtract_convert_fusion.1
  149.6 0.1 convert_bitcast_fusion
  149.7 0.3 broadcast_in_dim.8
  150.0 53.0 %all_to_all.24 = bf16[64,40,768]{2,1,0:T(8,128)(2,1)} all-to-all(bf16[64,40,768]{2,1,0:T(8,128)(2,1)S(1)} %broadcast_in_dim.8), channel_id=1, replica_groups=mesh['rep_hi'=8,'core'=2,'shard'=8] {'shard','rep_hi'}, dimensions={0} | all-to-all | bytes 7864320 | tf_op jit(solution)/shard_map/all_to_all | solution.py:32
  202.9 2.4 %collective-permute-start.1 = (bf16[64,40,768]{2,1,0:T(8,128)(2,1)}, bf16[64,40,768]{2,1,0:T(8,128)(2,1)}, u32[]{:S(2)}, u32[]{:S(2)}) collective-permute-start(bf16[64,40,768]{2,1,0:T(8,128)(2,1)} %all_to_all.24), channel_id=1, source_target_pairs={{0,8},{8,0},{1,9},{9,1},{2,10},{10,2},{3,11},{11,3},{4,12},{12,4},... | collective-permute-start | bytes 11796488 | tf_op jit(solution)/shard_map/ppermute | solution.py:126
  205.5 0.7 reshape.69
  206.1 0.8 select_bitcast_fusion.7
  206.9 0.2 select_bitcast_fusion.5
  207.0 0.7 slice_multiply_fusion.2
  207.8 0.1 mul.370
  207.8 1.1 maximum_multiply_fusion.1
  209.0 0.1 maximum_multiply_fusion
  209.1 0.1 copy.67
  209.3 0.6 multiply_subtract_fusion.2
  209.9 0.1 copy-done.4
  210.0 0.1 copy-done.5
  210.1 1.0 multiply_subtract_fusion.1
  211.2 0.8 copy-done
  212.0 3.0 %multiply_subtract_fusion = (f32[512,768]{1,0:T(8,128)}, f32[512,768]{1,0:T(8,128)}, f32[512,768]{1,0:T(8,128)}) fusion(f32[512,768]{1,0:T(8,128)S(1)} %copy-done, f32[8,2,32,768]{3,2,1,0:T(8,128)S(1)} %copy.67, f32[512,768]{1,0:T(8,128)S(1)} %copy-done.1, f32[512,768]{1,0:T(8,128)S(1)} %copy-done.2), kind=kLoop, calls=%fused_computation.13 | loop fusion | flops 5898240 | bytes 11010048 | tf_op jit(solution)/shard_map/sub | solution.py:26
  214.9 2.0 broadcast_select_fusion.1
  217.0 0.2 copy.71
  217.2 0.1 reshape.70
  217.3 0.1 reshape_squeeze.16
  217.4 0.7 reshape.71
  218.1 1.5 select_bitcast_fusion.3
  219.6 0.4 pad_maximum_fusion.1
  219.9 0.1 copy.70
  220.1 1.2 reshape_reshape.9
  221.3 3.1 %select_bitcast_fusion.1 = (bf16[64,1,32,768]{3,2,1,0:T(8,128)(2,1)S(1)}, bf16[64,1,32,768]{3,2,1,0:T(8,128)(2,1)S(1)}) fusion(pred[]{:T(512)S(6)} %eq.2, bf16[64,40,768]{2,1,0:T(8,128)(2,1)} %collective-permute-done.1, bf16[64,40,768]{2,1,0:T(8,128)(2,1)} %all_to_all.24), kind=kLoop, calls=%fused_computation.6 | loop fusion | flops 3145728 | bytes 12582913 | tf_op jit(solution)/shard_map/stack | solution.py:131
  224.4 3.3 %pad_maximum_fusion = bf16[64,2,32,768]{3,2,1,0:T(8,128)(2,1)} fusion(bf16[64,1,32,768]{3,2,1,0:T(8,128)(2,1)S(1)} %get-tuple-element.26, bf16[64,1,32,768]{3,2,1,0:T(8,128)(2,1)S(1)} %get-tuple-element.25), kind=kLoop, calls=%fused_computation.4 | loop fusion | flops 3145728 | bytes 12582912 | tf_op jit(solution)/shard_map/stack | solution.py:131
  (28 shorter events, 0.3 us)
Async XLA Ops:
  0.6 2.3 copy-start.9
  111.4 19.7 %copy-start.8 = (f32[4,96]{1,0:T(4,128)S(1)}, f32[4,96]{1,0:T(4,128)}, u32[]{:S(2)}) copy-start(f32[4,96]{1,0:T(4,128)} %param.21) | copy-start | bytes 4612
  111.4 19.7 %copy-start.7 = (f32[4,96]{1,0:T(4,128)S(1)}, f32[4,96]{1,0:T(4,128)}, u32[]{:S(2)}) copy-start(f32[4,96]{1,0:T(4,128)} %param.22) | copy-start | bytes 4612
  111.4 19.8 %copy-start.6 = (f32[4,96]{1,0:T(4,128)S(1)}, f32[4,96]{1,0:T(4,128)}, u32[]{:S(2)}) copy-start(f32[4,96]{1,0:T(4,128)} %param.23) | copy-start | bytes 4612
  129.5 3.8 %collective-permute-start = (f32[8,40,768]{2,1,0:T(8,128)S(1)}, f32[8,40,768]{2,1,0:T(8,128)S(1)}, u32[]{:S(2)}, u32[]{:S(2)}) collective-permute-start(f32[8,40,768]{2,1,0:T(8,128)S(1)} %all_to_all.22), channel_id=1, source_target_pairs={{0,8},{8,0},{1,9},{9,1},{2,10},{10,2},{3,11},{11,3},{4,12},{12,4},... | collective-permute-start | bytes 2949128 | tf_op jit(solution)/shard_map/ppermute | solution.py:82
  202.9 12.0 %collective-permute-start.1 = (bf16[64,40,768]{2,1,0:T(8,128)(2,1)}, bf16[64,40,768]{2,1,0:T(8,128)(2,1)}, u32[]{:S(2)}, u32[]{:S(2)}) collective-permute-start(bf16[64,40,768]{2,1,0:T(8,128)(2,1)} %all_to_all.24), channel_id=1, source_target_pairs={{0,8},{8,0},{1,9},{9,1},{2,10},{10,2},{3,11},{11,3},{4,12},{12,4},... | collective-permute-start | bytes 11796488 | tf_op jit(solution)/shard_map/ppermute | solution.py:126
  208.9 1.0 copy-start.3
  209.0 1.0 copy-start.4
  209.0 1.1 copy-start.5
  209.1 2.0 copy-start.1
  209.1 2.0 copy-start.2
  209.3 2.7 %copy-start = (f32[512,768]{1,0:T(8,128)S(1)}, f32[512,768]{1,0:T(8,128)}, u32[]{:S(2)}) copy-start(f32[512,768]{1,0:T(8,128)} %param.15) | copy-start | bytes 4718596

commit v6 on v5

--- a/solution.py
+++ b/solution.py
@@ -132,8 +132,13 @@
 
     embed_weights = interleave(0, e_rows).reshape(embed_rows, width)
     proj_weights = interleave(e_rows, e_rows + p_rows).reshape(proj_rows, width)
+    norm_mine, norm_other = w_mine[:, e_rows + p_rows, :n_vals], w_other[:, e_rows + p_rows, :n_vals]
+    norm_pair = [
+        jnp.where(core == 0, norm_mine, norm_other),
+        jnp.where(core == 0, norm_other, norm_mine),
+    ]
     norm_weights = (
-        interleave(e_rows + p_rows, e_rows + p_rows + 1)[:, 0, :n_vals]
+        jnp.stack(norm_pair, axis=1)
         .reshape(n_shard, norm_rows, block_norm)
         .transpose(1, 0, 2)
         .reshape(norm_rows, norm_cols)

time: 228 us -> 227 us (level)
    another operation x5 -> x4, other arithmetic: 8.22 us -> 8.2 us  [interleave(): return jnp.stack(pair, axis=1).reshape((n_all, hi - lo) + w_piece.shape[1:])]
where the time goes in v6:
time: 227 us; the launch traced here: 226 us
  blocking collectives  185 us (81%)
  other arithmetic  26.2 us (12%)
  local copies, waits for them, and re-layouts  7.1 us (3%)
  starting transfers between devices  3.99 us (2%)
  between operations  2.91 us (1%)
    all_to_all x1, blocking collectives, shards(): received = lax.all_to_all(send, ALL, 0, 0, tiled=True)  103 us
    all_to_all x3, blocking collectives, gather_all(): lax.all_to_all(jnp.broadcast_to(piece[None], (count,) + piece.shape), axi...  81.8 us
    another operation x4, other arithmetic, interleave(): return jnp.stack(pair, axis=1).reshape((n_all, hi - lo) + w_piece.shape[1:])  8.2 us
    sub x3, other arithmetic, adamw(): master_new = master - learning_rate * direction  4.63 us
  transfers between devices with their start and end apart: 2, of which 1 were waited for; matrix products, arithmetic and copies ran while one was open for 4% of the time, Pallas kernels for 0%

profile of v6, /device:TPU:1, one launch (start us, length us, event | category | flops | bytes accessed | tf_op | source)
XLA Modules:
  0.0 226.5 jit_solution(3907126469830571699)
XLA Ops:
  0.7 2.2 reshape_squeeze.11
  2.9 0.1 reshape_squeeze.12
  3.0 0.1 reshape.72
  3.1 3.8 %fusion.1 = bf16[128,40,768]{2,1,0:T(8,128)(2,1)S(1)} fusion(bf16[128,1,24]{2,1,0:T(2,128)(2,1)S(1)} %reshape.72, bf16[128,6,768]{2,1,0:T(8,128)(2,1)S(1)} %reshape_squeeze.11, bf16[128,32,768]{2,1,0:T(8,128)(2,1)} %bitcast.50), kind=kLoop, calls=%fused_computation.3 | loop fusion | flops 31457280 | bytes 15341568 | tf_op jit(solution)/shard_map/concatenate | solution.py:76
  6.9 103.4 %all_to_all.21 = bf16[128,40,768]{2,1,0:T(8,128)(2,1)S(1)} all-to-all(bf16[128,40,768]{2,1,0:T(8,128)(2,1)S(1)} %fusion.1), channel_id=1, replica_groups=mesh['rep_hi'=8,'core'=2,'shard'=8] {'shard','rep_hi','core'}, dimensions={0} | all-to-all | bytes 15728640 | tf_op jit(solution)/shard_map/all_to_all | solution.py:78
  110.3 1.1 convert_reduce_fusion
  111.4 0.1 broadcast_in_dim.6
  111.5 18.0 %all_to_all.22 = f32[8,40,768]{2,1,0:T(8,128)S(1)} all-to-all(f32[8,40,768]{2,1,0:T(8,128)S(1)} %broadcast_in_dim.6), channel_id=1, replica_groups=mesh['rep_hi'=8,'core'=2,'shard'=8] {'rep_hi'}, dimensions={0} | all-to-all | bytes 1966080 | tf_op jit(solution)/shard_map/all_to_all | solution.py:32
  129.5 1.6 collective-permute-start
  131.1 0.1 reshape.65
  131.2 0.1 reshape.66
  131.2 0.1 reshape.67
  131.3 0.9 multiply_reduce_fusion.1
  132.2 1.1 collective-permute-done
  133.3 0.8 multiply_reduce_fusion
  135.4 10.8 %all_to_all.23 = f32[8,1,1]{2,1,0:T(1,128)S(1)} all-to-all(f32[8,1,1]{2,1,0:T(1,128)S(1)} %broadcast_in_dim.7), channel_id=1, replica_groups=mesh['rep_hi'=8,'core'=2,'shard'=8] {'shard'}, dimensions={0} | all-to-all | bytes 64 | tf_op jit(solution)/shard_map/all_to_all | solution.py:32
  146.3 0.6 reduce_sum.39
  147.6 1.1 subtract_convert_fusion
  148.7 0.9 subtract_convert_fusion.1
  149.6 0.1 convert_bitcast_fusion
  149.7 0.3 broadcast_in_dim.8
  150.0 52.9 %all_to_all.24 = bf16[64,40,768]{2,1,0:T(8,128)(2,1)} all-to-all(bf16[64,40,768]{2,1,0:T(8,128)(2,1)S(1)} %broadcast_in_dim.8), channel_id=1, replica_groups=mesh['rep_hi'=8,'core'=2,'shard'=8] {'shard','rep_hi'}, dimensions={0} | all-to-all | bytes 7864320 | tf_op jit(solution)/shard_map/all_to_all | solution.py:32
  202.9 2.4 %collective-permute-start.1 = (bf16[64,40,768]{2,1,0:T(8,128)(2,1)}, bf16[64,40,768]{2,1,0:T(8,128)(2,1)}, u32[]{:S(2)}, u32[]{:S(2)}) collective-permute-start(bf16[64,40,768]{2,1,0:T(8,128)(2,1)} %all_to_all.24), channel_id=1, source_target_pairs={{0,8},{8,0},{1,9},{9,1},{2,10},{10,2},{3,11},{11,3},{4,12},{12,4},... | collective-permute-start | bytes 11796488 | tf_op jit(solution)/shard_map/ppermute | solution.py:126
  205.4 0.7 reshape.69
  206.1 0.8 select_bitcast_fusion.7
  206.9 0.2 select_bitcast_fusion.5
  207.0 0.7 slice_multiply_fusion.2
  207.7 0.1 mul.370
  207.8 1.1 maximum_multiply_fusion.1
  209.0 0.1 maximum_multiply_fusion
  209.1 0.1 copy.68
  209.3 0.6 multiply_subtract_fusion.2
  209.9 0.0 copy-done.3
  209.9 0.1 copy-done.4
  210.0 0.1 copy-done.5
  210.1 1.0 multiply_subtract_fusion.1
  211.2 0.8 copy-done
  212.0 3.0 %multiply_subtract_fusion = (f32[512,768]{1,0:T(8,128)}, f32[512,768]{1,0:T(8,128)}, f32[512,768]{1,0:T(8,128)}) fusion(f32[512,768]{1,0:T(8,128)S(1)} %copy-done, f32[8,2,32,768]{3,2,1,0:T(8,128)S(1)} %copy.68, f32[512,768]{1,0:T(8,128)S(1)} %copy-done.1, f32[512,768]{1,0:T(8,128)S(1)} %copy-done.2), kind=kLoop, calls=%fused_computation.13 | loop fusion | flops 5898240 | bytes 11010048 | tf_op jit(solution)/shard_map/sub | solution.py:26
  214.9 1.1 broadcast_select_fusion.1
  216.0 0.1 pad_maximum_fusion.3
  216.1 0.1 reshape.70
  216.2 0.7 reshape.71
  216.9 1.5 select_bitcast_fusion.3
  218.4 0.4 pad_maximum_fusion.1
  218.8 0.1 copy.71
  218.9 1.2 reshape_reshape.9
  220.1 3.1 %select_bitcast_fusion.1 = (bf16[64,1,32,768]{3,2,1,0:T(8,128)(2,1)S(1)}, bf16[64,1,32,768]{3,2,1,0:T(8,128)(2,1)S(1)}) fusion(pred[]{:T(512)S(6)} %eq.2, bf16[64,40,768]{2,1,0:T(8,128)(2,1)} %collective-permute-done.1, bf16[64,40,768]{2,1,0:T(8,128)(2,1)} %all_to_all.24), kind=kLoop, calls=%fused_computation.6 | loop fusion | flops 3145728 | bytes 12582913 | tf_op jit(solution)/shard_map/stack | solution.py:131
  223.2 3.3 %pad_maximum_fusion = bf16[64,2,32,768]{3,2,1,0:T(8,128)(2,1)} fusion(bf16[64,1,32,768]{3,2,1,0:T(8,128)(2,1)S(1)} %get-tuple-element.26, bf16[64,1,32,768]{3,2,1,0:T(8,128)(2,1)S(1)} %get-tuple-element.25), kind=kLoop, calls=%fused_computation.4 | loop fusion | flops 3145728 | bytes 12582912 | tf_op jit(solution)/shard_map/stack | solution.py:131
  (24 shorter events, 0.2 us)
Async XLA Ops:
  0.6 2.3 copy-start.9
  111.4 19.7 %copy-start.8 = (f32[4,96]{1,0:T(4,128)S(1)}, f32[4,96]{1,0:T(4,128)}, u32[]{:S(2)}) copy-start(f32[4,96]{1,0:T(4,128)} %param.21) | copy-start | bytes 4612
  111.4 19.7 %copy-start.7 = (f32[4,96]{1,0:T(4,128)S(1)}, f32[4,96]{1,0:T(4,128)}, u32[]{:S(2)}) copy-start(f32[4,96]{1,0:T(4,128)} %param.22) | copy-start | bytes 4612
  111.4 19.8 %copy-start.6 = (f32[4,96]{1,0:T(4,128)S(1)}, f32[4,96]{1,0:T(4,128)}, u32[]{:S(2)}) copy-start(f32[4,96]{1,0:T(4,128)} %param.23) | copy-start | bytes 4612
  129.5 3.8 %collective-permute-start = (f32[8,40,768]{2,1,0:T(8,128)S(1)}, f32[8,40,768]{2,1,0:T(8,128)S(1)}, u32[]{:S(2)}, u32[]{:S(2)}) collective-permute-start(f32[8,40,768]{2,1,0:T(8,128)S(1)} %all_to_all.22), channel_id=1, source_target_pairs={{0,8},{8,0},{1,9},{9,1},{2,10},{10,2},{3,11},{11,3},{4,12},{12,4},... | collective-permute-start | bytes 2949128 | tf_op jit(solution)/shard_map/ppermute | solution.py:82
  202.9 12.0 %collective-permute-start.1 = (bf16[64,40,768]{2,1,0:T(8,128)(2,1)}, bf16[64,40,768]{2,1,0:T(8,128)(2,1)}, u32[]{:S(2)}, u32[]{:S(2)}) collective-permute-start(bf16[64,40,768]{2,1,0:T(8,128)(2,1)} %all_to_all.24), channel_id=1, source_target_pairs={{0,8},{8,0},{1,9},{9,1},{2,10},{10,2},{3,11},{11,3},{4,12},{12,4},... | collective-permute-start | bytes 11796488 | tf_op jit(solution)/shard_map/ppermute | solution.py:126
  208.9 1.0 copy-start.3
  209.0 1.0 copy-start.4
  209.0 1.1 copy-start.5
  209.1 2.0 copy-start.1
  209.1 2.0 copy-start.2
  209.3 2.7 %copy-start = (f32[512,768]{1,0:T(8,128)S(1)}, f32[512,768]{1,0:T(8,128)}, u32[]{:S(2)}) copy-start(f32[512,768]{1,0:T(8,128)} %param.15) | copy-start | bytes 4718596
